TPU v7x, 128 devices: a whole 4x4x4 slice. The times are simulated.
128 devices in a mesh: row: 32 (over x_lo, z, y), col: 4 (over x_hi, core).
Axes of the slice: x: 4 (x_hi: 2, x_lo: 2; x = x_hi * 2 + x_lo), y: 4, z: 4, core: 2. Of those that a mesh axis runs over, the one named last changes fastest.
Arguments:
- inputs: bfloat16 [1024, 8192], P('row', 'col'), may hold values from -6 to 6
- out_grad: bfloat16 [1024, 8192], P('row', 'col'), may hold values from -4 to 4
- gate_pre: bfloat16 [1024, 28672], P('col', 'row'), may hold values from -6 to 6
- up_pre: bfloat16 [1024, 28672], P('col', 'row'), may hold values from -6 to 6
- gate_weight: bfloat16 [8192, 28672], P('col', 'row'), may hold values from -0.0625 to 0.0625
- up_weight: bfloat16 [8192, 28672], P('col', 'row'), may hold values from -0.0625 to 0.0625
- down_weight: bfloat16 [28672, 8192], P('row', 'col'), may hold values from -0.03125 to 0.03125
Outputs:
- grad_input: bfloat16 [1024, 8192], P('row', 'col')
- grad_gate: bfloat16 [8192, 28672], P('col', 'row')
- grad_up: bfloat16 [8192, 28672], P('col', 'row')
- grad_down: bfloat16 [28672, 8192], P('row', 'col')
All inputs are finite; a program needn't handle non-finite values.
Results may differ from a plain program's by a relative error of at most 0.005.
Values may be sent and summed in bfloat16 or wider, within the bound.
No kernel may reach another device: no remote copies, remote signals or barrier semaphores. Data moves between devices by JAX's collectives and lax.ppermute only.
A program may use at most 128 MiB of HBM per device.

v0:
```python
import jax
import jax.numpy as jnp
from jax import lax
from jax.sharding import PartitionSpec as P


def swiglu_back(hidden_grad, gate_stored, up_stored):
    gate_value = gate_stored.astype(jnp.float32)
    up_value = up_stored.astype(jnp.float32)
    sigmoid_gate = jax.nn.sigmoid(gate_value)
    activated = gate_value * sigmoid_gate
    hidden = (activated * up_value).astype(jnp.bfloat16)
    gate_grad = (
        hidden_grad * up_value * sigmoid_gate * (1.0 + gate_value * (1.0 - sigmoid_gate))
    ).astype(jnp.bfloat16)
    up_grad = (hidden_grad * activated).astype(jnp.bfloat16)
    return (hidden, gate_grad, up_grad)


def contract_last(left, right):
    return lax.dot_general(
        left, right, (((1,), (1,)), ((), ())), preferred_element_type=jnp.float32
    )


def contract_first(left, right):
    return lax.dot_general(
        left, right, (((0,), (0,)), ((), ())), preferred_element_type=jnp.float32
    )


def gather_rows(block, axis, count):
    tiled = jnp.tile(block, (count, 1))
    return lax.all_to_all(tiled, axis, 0, 0, tiled=True)


def scatter_sum_rows(partial, axis, count):
    received = lax.all_to_all(partial.astype(jnp.bfloat16), axis, 0, 0, tiled=True)
    received = received.reshape((count, partial.shape[0] // count) + partial.shape[1:])
    return received.astype(jnp.float32).sum(0)


def sum_all(partial, axis, count):
    received = lax.all_to_all(partial, axis, 0, 0, tiled=True)
    total = received.reshape((count, partial.shape[0] // count) + partial.shape[1:]).sum(0)
    return gather_rows(total, axis, count)


def make_body(rows, cols):
    def body(inputs, out_grad, gate_pre, up_pre, gate_weight, up_weight, down_weight):
      grad_rows = gather_rows(out_grad, "row", rows)
      width = gate_pre.shape[1]
      pre_all = lax.all_gather(
          jnp.concatenate([gate_pre, up_pre], axis=1), "col", axis=0, tiled=True
      )
      gate_all, up_all = pre_all[:, :width], pre_all[:, width:]
      partial_hidden = contract_last(grad_rows, down_weight)
      hidden_total = sum_all(partial_hidden, "col", cols)
      hidden, gate_grad, up_grad = swiglu_back(hidden_total, gate_all, up_all)
      grad_down = contract_first(hidden, grad_rows).astype(jnp.bfloat16)
      input_rows = lax.all_gather(inputs, "row", axis=0, tiled=True)
      gate_total = contract_first(input_rows, gate_grad)
      up_total = contract_first(input_rows, up_grad)
      input_total = scatter_sum_rows(
          contract_last(gate_grad, gate_weight) + contract_last(up_grad, up_weight),
          "row",
          rows,
      )
      return (
          input_total.astype(jnp.bfloat16),
          gate_total.astype(jnp.bfloat16),
          up_total.astype(jnp.bfloat16),
          grad_down,
      )

    return body


def solution(mesh):
    in_specs = (
        P("row", "col"),
        P("row", "col"),
        P("col", "row"),
        P("col", "row"),
        P("col", "row"),
        P("col", "row"),
        P("row", "col"),
    )
    out_specs = (P("row", "col"), P("col", "row"), P("col", "row"), P("row", "col"))
    body = make_body(mesh.shape["row"], mesh.shape["col"])
    return jax.shard_map(body, mesh=mesh, in_specs=in_specs, out_specs=out_specs, check_vma=False)
```

profile of v0, /device:TPU:4, one launch (start us, length us, event | category | flops | bytes accessed | tf_op | source)
XLA Modules:
  0.0 337.8 jit_solution(8116195541101035508)
XLA Ops:
  7.2 3.4 %tile.4 = bf16[32,32,2048]{2,1,0:T(8,128)(2,1)} broadcast(bf16[32,2048]{1,0:T(8,128)(2,1)} %param.8), dimensions={1,2} | broadcast | bytes 4325376 | tf_op jit(solution)/shard_map/tile | solution.py:33
  10.6 0.0 copy-start.1
  10.6 0.0 copy-start.2
  10.6 9.2 %all-to-all-start = ((bf16[32,32,2048]{2,1,0:T(8,128)(2,1)}), bf16[32,32,2048]{2,1,0:T(8,128)(2,1)}, u32[]{:S(2)}, u32[]{:S(2)}) async-start(bf16[32,32,2048]{2,1,0:T(8,128)(2,1)} %tile.4), calls=%async_computation | async-start | bytes 8388608 | tf_op jit(solution)/shard_map/all_to_all | solution.py:34
  19.8 0.0 all-gather.3.cloned.1.call-start
  19.9 0.0 copy-done.1
  19.9 0.0 copy-done.2
  19.9 1.0 pad_maximum_fusion
  20.9 0.0 all-gather.3.cloned.1.call-update
  20.9 67.6 %all-to-all-done = bf16[32,32,2048]{2,1,0:T(8,128)(2,1)} async-done(((bf16[32,32,2048]{2,1,0:T(8,128)(2,1)}), bf16[32,32,2048]{2,1,0:T(8,128)(2,1)}, u32[]{:S(2)}, u32[]{:S(2)}) %all-to-all-start) | async-done | bytes 4194336 | tf_op jit(solution)/shard_map/all_to_all | solution.py:34
  88.5 9.7 %fusion.9 = f32[4,256,896]{2,1,0:T(8,128)} fusion(bf16[4,256,2048]{2,1,0:T(8,128)(2,1)} %bitcast, bf16[896,2048]{1,0:T(8,128)(2,1)} %param.13), kind=kOutput, calls=%fused_computation.16 | convolution fusion | flops 3758096384 | bytes 11534336 | tf_op jit(solution)/shard_map/dot_general | solution.py:21
  98.2 5.6 %all-to-all-start.1 = ((f32[4,256,896]{2,1,0:T(8,128)}), f32[4,256,896]{2,1,0:T(8,128)}, u32[]{:S(2)}, u32[]{:S(2)}) async-start(f32[4,256,896]{2,1,0:T(8,128)} %fusion.9), calls=%async_computation.1 | async-start | bytes 7340032 | tf_op jit(solution)/shard_map/all_to_all | solution.py:44
  103.8 0.0 all-gather.5.cloned.1.call-start
  103.8 0.7 all-gather.5.cloned.1.call-update
  104.5 51.7 %all-to-all-done.1 = f32[4,256,896]{2,1,0:T(8,128)} async-done(((f32[4,256,896]{2,1,0:T(8,128)}), f32[4,256,896]{2,1,0:T(8,128)}, u32[]{:S(2)}, u32[]{:S(2)}) %all-to-all-start.1) | async-done | bytes 3670048 | tf_op jit(solution)/shard_map/all_to_all | solution.py:44
  156.2 2.3 reduce_sum.21
  158.5 2.1 tile.5
  160.6 8.0 %all-to-all-start.2 = ((f32[4,256,896]{2,1,0:T(8,128)}), f32[4,256,896]{2,1,0:T(8,128)}, u32[]{:S(2)}, u32[]{:S(2)}) async-start(f32[4,256,896]{2,1,0:T(8,128)} %tile.5), calls=%async_computation.2 | async-start | bytes 7340032 | tf_op jit(solution)/shard_map/all_to_all | solution.py:34
  168.6 0.0 all-gather.3.cloned.1.call-done
  168.6 58.0 %all-to-all-done.2 = f32[4,256,896]{2,1,0:T(8,128)} async-done(((f32[4,256,896]{2,1,0:T(8,128)}), f32[4,256,896]{2,1,0:T(8,128)}, u32[]{:S(2)}, u32[]{:S(2)}) %all-to-all-start.2) | async-done | bytes 3670048 | tf_op jit(solution)/shard_map/all_to_all | solution.py:34
  226.6 0.0 copy-start.3
  226.6 4.2 %fusion.8 = (bf16[1024,896]{1,0:T(8,128)(2,1)S(1)}, bf16[1024,896]{1,0:T(8,128)(2,1)S(1)}) fusion(f32[4,256,896]{2,1,0:T(8,128)} %all-to-all-done.2, bf16[1024,1792]{1,0:T(8,128)(2,1)} %all-gather.3.cloned.1.call-done), kind=kLoop, calls=%fused_computation.15 | loop fusion | flops 13762560 | bytes 11010048 | tf_op jit(solution)/shard_map/convert_element_type | solution.py:16
  230.8 0.0 copy-start
  230.8 0.0 copy-done.3
  230.8 0.0 copy-start.4
  230.8 4.5 %fusion.14 = f32[1024,2048]{1,0:T(8,128)S(1)} fusion(bf16[1024,896]{1,0:T(8,128)(2,1)S(1)} %get-tuple-element.9, bf16[2048,896]{1,0:T(8,128)(2,1)S(1)} %copy-done.3), kind=kOutput, calls=%fused_computation.24 | convolution fusion | flops 3758096384 | bytes 13893632 | tf_op jit(solution)/shard_map/dot_general | solution.py:21
  235.3 0.0 copy-done
  235.4 0.0 copy-done.4
  235.4 6.2 %add_convert_fusion = bf16[1024,2048]{1,0:T(8,128)(2,1)} fusion(f32[1024,2048]{1,0:T(8,128)S(1)} %fusion.14, bf16[1024,896]{1,0:T(8,128)(2,1)S(1)} %get-tuple-element.8, bf16[2048,896]{1,0:T(8,128)(2,1)S(1)} %copy-done.4), kind=kOutput, calls=%fused_computation | convolution fusion | flops 3762290688 | bytes 18087936 | tf_op jit(solution)/shard_map/dot_general | solution.py:21
  241.6 8.0 %all-to-all-start.3 = ((bf16[32,32,2048]{2,1,0:T(8,128)(2,1)}), bf16[32,32,2048]{2,1,0:T(8,128)(2,1)}, u32[]{:S(2)}, u32[]{:S(2)}) async-start(bf16[32,32,2048]{2,1,0:T(8,128)(2,1)} %bitcast.25), calls=%async_computation.3 | async-start | bytes 8388608 | tf_op jit(solution)/shard_map/all_to_all | solution.py:38
  249.5 9.4 %convolution_convert_fusion = bf16[896,2048]{1,0:T(8,128)(2,1)} fusion(bf16[1024,2048]{1,0:T(8,128)(2,1)} %bitcast.6, bf16[1024,1792]{1,0:T(8,128)(2,1)} %all-gather.3.cloned.1.call-done), kind=kOutput, calls=%fused_computation.20 | convolution fusion | flops 3767271424 | bytes 11534336 | tf_op jit(solution)/shard_map/dot_general | solution.py:27
  259.0 39.6 %all-gather.5.cloned.1.call-done = bf16[1024,2048]{1,0:T(8,128)(2,1)} async-done(((bf16[32,2048]{1,0:T(8,128)(2,1)}), bf16[1024,2048]{1,0:T(8,128)(2,1)}) %all-gather.5.cloned.1.call-update) | async-done | bytes 4194320 | tf_op jit(solution)/shard_map/all_gather | solution.py:61
  298.6 8.6 %convert_bitcast_fusion.1 = bf16[2048,896]{0,1:T(8,128)(2,1)} fusion(bf16[1024,896]{1,0:T(8,128)(2,1)} %copy-done, bf16[1024,2048]{1,0:T(8,128)(2,1)} %all-gather.5.cloned.1.call-done), kind=kOutput, calls=%fused_computation.19 | convolution fusion | flops 3759931392 | bytes 9699328 | tf_op jit(solution)/shard_map/dot_general | solution.py:27
  307.2 6.0 %copy.11 = bf16[2048,896]{1,0:T(8,128)(2,1)} copy(bf16[2048,896]{0,1:T(8,128)(2,1)} %convert_bitcast_fusion.1) | data formatting | bytes 7340032
  313.2 8.0 %convert_bitcast_fusion = bf16[2048,896]{0,1:T(8,128)(2,1)} fusion(bf16[1024,896]{1,0:T(8,128)(2,1)S(1)} %get-tuple-element.8, bf16[1024,2048]{1,0:T(8,128)(2,1)} %all-gather.5.cloned.1.call-done), kind=kOutput, calls=%fused_computation.18 | convolution fusion | flops 3759931392 | bytes 9699328 | tf_op jit(solution)/shard_map/dot_general | solution.py:27
  321.2 6.0 %copy.12 = bf16[2048,896]{1,0:T(8,128)(2,1)} copy(bf16[2048,896]{0,1:T(8,128)(2,1)} %convert_bitcast_fusion) | data formatting | bytes 7340032
  327.3 0.0 all-to-all-done.3
  327.3 3.7 %reduce_sum.22 = bf16[32,2048]{1,0:T(8,128)(2,1)} reduce(bf16[32,32,2048]{2,1,0:T(8,128)(2,1)} %all-to-all-done.3, bf16[]{:T(256)} %constant.5.clone.1), dimensions={0}, to_apply=%region_1.0 | reduce | flops 2031616 | bytes 4325378 | tf_op jit(solution)/shard_map/reduce_sum | solution.py:40
Async XLA Ops:
  10.6 9.3 %copy-start.1 = (bf16[256,896]{1,0:T(8,128)(2,1)S(1)}, bf16[256,896]{1,0:T(8,128)(2,1)}, u32[]{:S(2)}) copy-start(bf16[256,896]{1,0:T(8,128)(2,1)} %param.10) | copy-start | bytes 1376260
  10.6 9.3 %copy-start.2 = (bf16[256,896]{1,0:T(8,128)(2,1)S(1)}, bf16[256,896]{1,0:T(8,128)(2,1)}, u32[]{:S(2)}) copy-start(bf16[256,896]{1,0:T(8,128)(2,1)} %param.9) | copy-start | bytes 1376260
  10.6 78.0 %all-to-all-start = ((bf16[32,32,2048]{2,1,0:T(8,128)(2,1)}), bf16[32,32,2048]{2,1,0:T(8,128)(2,1)}, u32[]{:S(2)}, u32[]{:S(2)}) async-start(bf16[32,32,2048]{2,1,0:T(8,128)(2,1)} %tile.4), calls=%async_computation | async-start | bytes 8388608 | tf_op jit(solution)/shard_map/all_to_all | solution.py:34
  19.8 148.8 %all-gather.3.cloned.1.call-start = ((), (), s32[]{:S(2)}) async-start(), calls=%async_computation.4 | async-start | bytes 4587520 | tf_op jit(solution)/shard_map/all_gather | solution.py:53
  98.2 58.0 %all-to-all-start.1 = ((f32[4,256,896]{2,1,0:T(8,128)}), f32[4,256,896]{2,1,0:T(8,128)}, u32[]{:S(2)}, u32[]{:S(2)}) async-start(f32[4,256,896]{2,1,0:T(8,128)} %fusion.9), calls=%async_computation.1 | async-start | bytes 7340032 | tf_op jit(solution)/shard_map/all_to_all | solution.py:44
  103.8 194.8 %all-gather.5.cloned.1.call-start = ((), (), s32[]{:S(2)}) async-start(), calls=%async_computation.5 | async-start | bytes 4325376 | tf_op jit(solution)/shard_map/all_gather | solution.py:61
  160.6 65.9 %all-to-all-start.2 = ((f32[4,256,896]{2,1,0:T(8,128)}), f32[4,256,896]{2,1,0:T(8,128)}, u32[]{:S(2)}, u32[]{:S(2)}) async-start(f32[4,256,896]{2,1,0:T(8,128)} %tile.5), calls=%async_computation.2 | async-start | bytes 7340032 | tf_op jit(solution)/shard_map/all_to_all | solution.py:34
  226.6 4.3 %copy-start.3 = (bf16[2048,896]{1,0:T(8,128)(2,1)S(1)}, bf16[2048,896]{1,0:T(8,128)(2,1)}, u32[]{:S(2)}) copy-start(bf16[2048,896]{1,0:T(8,128)(2,1)} %param.11) | copy-start | bytes 11010052
  230.8 4.6 %copy-start = (bf16[1024,896]{1,0:T(8,128)(2,1)}, bf16[1024,896]{1,0:T(8,128)(2,1)S(1)}, u32[]{:S(2)}) copy-start(bf16[1024,896]{1,0:T(8,128)(2,1)S(1)} %get-tuple-element.9) | copy-start | bytes 5505028
  230.8 4.5 %copy-start.4 = (bf16[2048,896]{1,0:T(8,128)(2,1)S(1)}, bf16[2048,896]{1,0:T(8,128)(2,1)}, u32[]{:S(2)}) copy-start(bf16[2048,896]{1,0:T(8,128)(2,1)} %param.12) | copy-start | bytes 11010052
  241.6 85.7 %all-to-all-start.3 = ((bf16[32,32,2048]{2,1,0:T(8,128)(2,1)}), bf16[32,32,2048]{2,1,0:T(8,128)(2,1)}, u32[]{:S(2)}, u32[]{:S(2)}) async-start(bf16[32,32,2048]{2,1,0:T(8,128)(2,1)} %bitcast.25), calls=%async_computation.3 | async-start | bytes 8388608 | tf_op jit(solution)/shard_map/all_to_all | solution.py:38
Sparse Core Ops, SparseCore 0:
  22.9 54.0 all-gather.2
  106.2 192.3 all-gather.4
where the time goes:
time: 339 us; the launch traced here: 338 us
  waiting for transfers between devices  218 us (64%)
  matrix products  46.4 us (14%)
  starting transfers between devices  30.8 us (9%)
  local copies, waits for them, and re-layouts  17.6 us (5%)
  between operations  14.1 us (4%)
  other arithmetic  11.2 us (3%)
    all_to_all x2, waiting for transfers between devices, gather_rows(): return lax.all_to_all(tiled, axis, 0, 0, tiled=True)  126 us
    all_to_all x1, waiting for transfers between devices, sum_all(): received = lax.all_to_all(partial, axis, 0, 0, tiled=True)  51.7 us
    all_gather x1, waiting for transfers between devices, body(): input_rows = lax.all_gather(inputs, 'row', axis=0, tiled=True)  39.6 us
    dot_general x3, matrix products, contract_first(): lax.dot_general(left, right, (((0,), (0,)), ((), ())), preferred_element_...  26 us
    dot_general x3, matrix products, contract_last(): lax.dot_general(left, right, (((1,), (1,)), ((), ())), preferred_element_...  20.4 us
    all_to_all x2, starting transfers between devices, gather_rows(): return lax.all_to_all(tiled, axis, 0, 0, tiled=True)  17.2 us
    unnamed x12, local copies, waits for them, and re-layouts  12.2 us
    all_to_all x1, starting transfers between devices, scatter_sum_rows(): lax.all_to_all(partial.astype(jnp.bfloat16), axis, 0, 0, tiled=True)  7.98 us
  transfers between devices with their start and end apart: 6, of which 4 were waited for; matrix products, arithmetic and copies ran while one was open for 20% of the time, Pallas kernels for 0%

commit v1 on v0

--- a/solution.py
+++ b/solution.py
@@ -40,15 +40,39 @@
     return received.astype(jnp.float32).sum(0)
 
 
+def swap(value, axis, count, bit):
+    pairs = [(i, i ^ bit) for i in range(count)]
+    return lax.ppermute(value, axis, pairs)
+
+
+def halve_sum(value, axis, count, bit, own):
+    half = value.shape[0] // 2
+    keep = lax.dynamic_slice_in_dim(value, own * half, half, axis=0)
+    give = lax.dynamic_slice_in_dim(value, (1 - own) * half, half, axis=0)
+    return keep + swap(give, axis, count, bit)
+
+
+def double(value, axis, count, bit, own):
+    other = swap(value, axis, count, bit)
+    first = jnp.where(own == 0, value, other)
+    second = jnp.where(own == 0, other, value)
+    return jnp.concatenate([first, second], axis=0)
+
+
 def sum_all(partial, axis, count):
-    received = lax.all_to_all(partial, axis, 0, 0, tiled=True)
-    total = received.reshape((count, partial.shape[0] // count) + partial.shape[1:]).sum(0)
-    return gather_rows(total, axis, count)
+    index = lax.axis_index(axis)
+    near, far = index % 2, (index // 2) % 2
+    total = halve_sum(partial, axis, count, 1, near)
+    total = halve_sum(total, axis, count, 2, far)
+    total = double(total, axis, count, 2, far)
+    return double(total, axis, count, 1, near)
 
 
 def make_body(rows, cols):
     def body(inputs, out_grad, gate_pre, up_pre, gate_weight, up_weight, down_weight):
-      grad_rows = gather_rows(out_grad, "row", rows)
+      features = out_grad.shape[1]
+      both_rows = gather_rows(jnp.concatenate([out_grad, inputs], axis=1), "row", rows)
+      grad_rows, input_rows = both_rows[:, :features], both_rows[:, features:]
       width = gate_pre.shape[1]
       pre_all = lax.all_gather(
           jnp.concatenate([gate_pre, up_pre], axis=1), "col", axis=0, tiled=True
@@ -58,7 +82,6 @@
       hidden_total = sum_all(partial_hidden, "col", cols)
       hidden, gate_grad, up_grad = swiglu_back(hidden_total, gate_all, up_all)
       grad_down = contract_first(hidden, grad_rows).astype(jnp.bfloat16)
-      input_rows = lax.all_gather(inputs, "row", axis=0, tiled=True)
       gate_total = contract_first(input_rows, gate_grad)
       up_total = contract_first(input_rows, up_grad)
       input_total = scatter_sum_rows(

time: 339 us -> 340 us (level)
  the two profiles are of different devices: /device:TPU:4 before, /device:TPU:2 now
where the time goes in v1:
time: 340 us
  waiting for transfers between devices  217 us (64%)
  matrix products  50.4 us (15%)
  starting transfers between devices  30.9 us (9%)
  other arithmetic  20.2 us (6%)
  between operations  14.2 us (4%)
  local copies, waits for them, and re-layouts  7.27 us (2%)
    all_to_all x1, waiting for transfers between devices, gather_rows(): return lax.all_to_all(tiled, axis, 0, 0, tiled=True)  122 us
    ppermute x4, waiting for transfers between devices, swap(): return lax.ppermute(value, axis, pairs)  63.1 us
    all_to_all x1, waiting for transfers between devices, scatter_sum_rows(): lax.all_to_all(partial.astype(jnp.bfloat16), axis, 0, 0, tiled=True)  31.3 us
    dot_general x3, matrix products, contract_first(): lax.dot_general(left, right, (((0,), (0,)), ((), ())), preferred_element_...  26.2 us
    dot_general x3, matrix products, contract_last(): lax.dot_general(left, right, (((1,), (1,)), ((), ())), preferred_element_...  24.1 us
    all_to_all x1, starting transfers between devices, scatter_sum_rows(): lax.all_to_all(partial.astype(jnp.bfloat16), axis, 0, 0, tiled=True)  16.1 us
    all_to_all x1, starting transfers between devices, gather_rows(): return lax.all_to_all(tiled, axis, 0, 0, tiled=True)  9.62 us
  transfers between devices with their start and end apart: 7, of which 6 were waited for; matrix products, arithmetic and copies ran while one was open for 11% of the time, Pallas kernels for 0%

profile of v1, /device:TPU:2, one launch (start us, length us, event | category | flops | bytes accessed | tf_op | source)
XLA Modules:
  0.0 339.5 jit_solution(16792536054911144328)
XLA Ops:
  7.2 1.0 pad_maximum_fusion.3
  8.2 4.3 %tile.2 = bf16[32,32,4096]{2,1,0:T(8,128)(2,1)} broadcast(bf16[32,4096]{1,0:T(8,128)(2,1)S(1)} %pad_maximum_fusion.3), dimensions={1,2} | broadcast | bytes 8650752 | tf_op jit(solution)/shard_map/tile | solution.py:33
  12.4 9.6 %all-to-all-start = ((bf16[32,32,4096]{2,1,0:T(8,128)(2,1)}), bf16[32,32,4096]{2,1,0:T(8,128)(2,1)}, u32[]{:S(2)}, u32[]{:S(2)}) async-start(bf16[32,32,4096]{2,1,0:T(8,128)(2,1)} %tile.2), calls=%async_computation | async-start | bytes 16777216 | tf_op jit(solution)/shard_map/all_to_all | solution.py:34
  22.1 0.0 all-gather.2.cloned.1.call-start
  22.1 122.2 %all-to-all-done = bf16[32,32,4096]{2,1,0:T(8,128)(2,1)} async-done(((bf16[32,32,4096]{2,1,0:T(8,128)(2,1)}), bf16[32,32,4096]{2,1,0:T(8,128)(2,1)}, u32[]{:S(2)}, u32[]{:S(2)}) %all-to-all-start) | async-done | bytes 8388640 | tf_op jit(solution)/shard_map/all_to_all | solution.py:34
  144.3 7.4 %fusion.6 = f32[1024,896]{1,0:T(8,128)S(1)} fusion(bf16[896,2048]{1,0:T(8,128)(2,1)} %param.13, bf16[1024,4096]{1,0:T(8,128)(2,1)} %bitcast), kind=kOutput, calls=%fused_computation.12 | convolution fusion | flops 3758096384 | bytes 11534336 | tf_op jit(solution)/shard_map/dot_general | solution.py:21
  151.8 0.0 copy-start.5
  151.8 1.8 copy-done.5
  153.6 0.0 copy-start.8
  153.6 0.0 copy-start.9
  153.6 0.1 constant_dynamic-slice_fusion.1
  153.7 0.1 collective-permute-start
  153.8 0.8 copy-done.8
  154.6 0.1 copy-done.9
  154.8 1.0 pad_maximum_fusion.2
  155.8 0.0 all-gather.2.cloned.1.call-update
  155.8 1.9 collective-permute-done
  157.7 2.2 dynamic-slice_add_fusion
  160.0 0.1 constant_dynamic-slice_fusion
  160.0 2.2 collective-permute-start.1
  162.3 28.9 %collective-permute-done.1 = f32[256,896]{1,0:T(8,128)} collective-permute-done((f32[256,896]{1,0:T(8,128)S(1)}, f32[256,896]{1,0:T(8,128)}, u32[]{:S(2)}, u32[]{:S(2)}) %collective-permute-start.1) | collective-permute-done | bytes 917536 | tf_op jit(solution)/shard_map/ppermute | solution.py:45
  191.1 1.3 dynamic-slice_add_fusion.1
  192.4 2.9 collective-permute-start.2
  195.3 28.1 %collective-permute-done.2 = f32[256,896]{1,0:T(8,128)} collective-permute-done((f32[256,896]{1,0:T(8,128)S(1)}, f32[256,896]{1,0:T(8,128)}, u32[]{:S(2)}, u32[]{:S(2)}) %collective-permute-start.2) | collective-permute-done | bytes 917536 | tf_op jit(solution)/shard_map/ppermute | solution.py:45
  223.5 1.3 broadcast_select_fusion.3
  224.8 1.3 pad_maximum_fusion.1
  226.1 0.0 collective-permute-start.3
  226.1 4.1 %collective-permute-done.3 = f32[512,896]{1,0:T(8,128)} collective-permute-done((f32[512,896]{1,0:T(8,128)}, f32[512,896]{1,0:T(8,128)}, u32[]{:S(2)}, u32[]{:S(2)}) %collective-permute-start.3) | collective-permute-done | bytes 1835040 | tf_op jit(solution)/shard_map/ppermute | solution.py:45
  230.2 3.6 %broadcast_select_fusion.1 = (f32[512,896]{1,0:T(8,128)}, f32[512,896]{1,0:T(8,128)}) fusion(f32[512,896]{1,0:T(8,128)} %collective-permute-done.3, pred[]{:T(512)S(6)} %eq.11, f32[256,896]{1,0:T(8,128)S(1)} %get-tuple-element.7, f32[256,896]{1,0:T(8,128)S(1)} %get-tuple-element.6), kind=kLoop, calls=%fused_computation.33 | loop fusion | flops 1376256 | bytes 7340033 | tf_op jit(solution)/shard_map/jit(_where)/select_n | solution.py:57
  233.8 0.0 all-gather.2.cloned.1.call-done
  233.8 0.0 copy-start.10
  233.8 4.8 %fusion.10 = bf16[1024,896]{1,0:T(8,128)(2,1)S(1)} fusion(f32[512,896]{1,0:T(8,128)} %get-tuple-element.5, f32[512,896]{1,0:T(8,128)} %get-tuple-element.4, bf16[1024,1792]{1,0:T(8,128)(2,1)} %all-gather.2.cloned.1.call-done), kind=kLoop, calls=%fused_computation.16 | loop fusion | flops 11927552 | bytes 9175040 | tf_op jit(solution)/shard_map/convert_element_type | solution.py:15
  238.6 0.0 copy-done.10
  238.7 0.0 copy-start.6
  238.7 0.0 copy-start
  238.7 0.0 copy-start.1
  238.7 0.0 copy-start.3
  238.7 6.7 %fusion.28 = f32[1024,2048]{1,0:T(8,128)} fusion(bf16[1024,896]{1,0:T(8,128)(2,1)S(1)} %fusion.10, bf16[2048,896]{1,0:T(8,128)(2,1)S(1)} %copy-done.10), kind=kOutput, calls=%fused_computation.40 | convolution fusion | flops 3758096384 | bytes 13893632 | tf_op jit(solution)/shard_map/dot_general | solution.py:21
  245.4 0.0 copy-done.6
  245.4 0.0 copy-done
  245.4 0.0 copy-done.1
  245.4 0.0 copy-done.3
  245.4 10.0 %add_convert_fusion = bf16[1024,2048]{1,0:T(8,128)(2,1)} fusion(f32[1024,2048]{1,0:T(8,128)} %fusion.28, bf16[2048,896]{1,0:T(8,128)(2,1)} %param.12, f32[512,896]{1,0:T(8,128)S(1)} %copy-done.1, f32[512,896]{1,0:T(8,128)S(1)} %copy-done, bf16[1024,1792]{1,0:T(8,128)(2,1)S(1)} %copy-done.3), kind=kOutput, calls=%fused_computation | convolution fusion | flops 3769630720 | bytes 21757952 | tf_op jit(solution)/shard_map/dot_general | solution.py:21
  255.4 16.1 %all-to-all-start.1 = ((bf16[32,32,2048]{2,1,0:T(8,128)(2,1)}), bf16[32,32,2048]{2,1,0:T(8,128)(2,1)}, u32[]{:S(2)}, u32[]{:S(2)}) async-start(bf16[32,32,2048]{2,1,0:T(8,128)(2,1)} %bitcast.7), calls=%async_computation.1 | async-start | bytes 8388608 | tf_op jit(solution)/shard_map/all_to_all | solution.py:38
  271.5 0.0 copy-start.7
  271.5 9.5 %fusion.16 = bf16[896,2048]{1,0:T(8,128)(2,1)} fusion(bf16[1024,4096]{1,0:T(8,128)(2,1)} %bitcast, bf16[1024,1792]{1,0:T(8,128)(2,1)} %all-gather.2.cloned.1.call-done), kind=kOutput, calls=%fused_computation.24 | convolution fusion | flops 3767271424 | bytes 11534336 | tf_op jit(solution)/shard_map/dot_general | solution.py:27
  281.0 0.0 copy-done.7
  281.0 0.0 copy-start.2
  281.0 0.0 copy-start.4
  281.0 8.3 %fusion.19 = bf16[2048,896]{1,0:T(8,128)(2,1)} fusion(bf16[1024,896]{1,0:T(8,128)(2,1)S(1)} %copy-done.7, bf16[1024,4096]{1,0:T(8,128)(2,1)} %bitcast), kind=kOutput, calls=%fused_computation.25 | convolution fusion | flops 3759931392 | bytes 9699328 | tf_op jit(solution)/shard_map/dot_general | solution.py:27
  289.3 0.0 copy-done.2
  289.3 0.0 copy-done.4
  289.3 8.4 %fusion.22 = bf16[2048,896]{1,0:T(8,128)(2,1)} fusion(bf16[1024,4096]{1,0:T(8,128)(2,1)} %bitcast, f32[512,896]{1,0:T(8,128)S(1)} %copy-done.2, f32[512,896]{1,0:T(8,128)S(1)} %copy-done, bf16[1024,1792]{1,0:T(8,128)(2,1)S(1)} %copy-done.4), kind=kOutput, calls=%fused_computation.26 | convolution fusion | flops 3767271424 | bytes 13369344 | tf_op jit(solution)/shard_map/dot_general | solution.py:27
  297.7 31.3 %all-to-all-done.1 = bf16[32,32,2048]{2,1,0:T(8,128)(2,1)} async-done(((bf16[32,32,2048]{2,1,0:T(8,128)(2,1)}), bf16[32,32,2048]{2,1,0:T(8,128)(2,1)}, u32[]{:S(2)}, u32[]{:S(2)}) %all-to-all-start.1) | async-done | bytes 4194336 | tf_op jit(solution)/shard_map/all_to_all | solution.py:38
  329.0 3.7 %reduce_sum.12 = bf16[32,2048]{1,0:T(8,128)(2,1)} reduce(bf16[32,32,2048]{2,1,0:T(8,128)(2,1)} %all-to-all-done.1, bf16[]{:T(256)} %constant.44.clone.1), dimensions={0}, to_apply=%region_0.1 | reduce | flops 2031616 | bytes 4325378 | tf_op jit(solution)/shard_map/reduce_sum | solution.py:40
Async XLA Ops:
  12.4 131.9 %all-to-all-start = ((bf16[32,32,4096]{2,1,0:T(8,128)(2,1)}), bf16[32,32,4096]{2,1,0:T(8,128)(2,1)}, u32[]{:S(2)}, u32[]{:S(2)}) async-start(bf16[32,32,4096]{2,1,0:T(8,128)(2,1)} %tile.2), calls=%async_computation | async-start | bytes 16777216 | tf_op jit(solution)/shard_map/all_to_all | solution.py:34
  22.1 211.7 %all-gather.2.cloned.1.call-start = ((), (), s32[]{:S(2)}) async-start(), calls=%async_computation.2 | async-start | bytes 4587520 | tf_op jit(solution)/shard_map/all_gather | solution.py:77
  151.8 1.8 copy-start.5
  153.6 1.0 copy-start.8
  153.6 1.2 copy-start.9
  153.7 4.0 %collective-permute-start = (f32[512,896]{1,0:T(8,128)S(1)}, f32[512,896]{1,0:T(8,128)}, u32[]{:S(2)}, u32[]{:S(2)}) collective-permute-start(f32[512,896]{1,0:T(8,128)S(1)} %constant_dynamic-slice_fusion.1), channel_id=1, source_target_pairs={{0,1},{1,0},{2,3},{3,2},{4,5},{5,4},{6,7},{7,6},{8,9},{9,8},{10,11... | collective-permute-start | bytes 5505032 | tf_op jit(solution)/shard_map/ppermute | solution.py:45
  160.0 31.1 %collective-permute-start.1 = (f32[256,896]{1,0:T(8,128)S(1)}, f32[256,896]{1,0:T(8,128)}, u32[]{:S(2)}, u32[]{:S(2)}) collective-permute-start(f32[256,896]{1,0:T(8,128)S(1)} %constant_dynamic-slice_fusion), channel_id=1, source_target_pairs={{0,2},{1,3},{2,0},{3,1},{4,6},{5,7},{6,4},{7,5},{8,10},{9,11},{10,... | collective-permute-start | bytes 2752520 | tf_op jit(solution)/shard_map/ppermute | solution.py:45
  192.4 31.0 %collective-permute-start.2 = (f32[256,896]{1,0:T(8,128)S(1)}, f32[256,896]{1,0:T(8,128)}, u32[]{:S(2)}, u32[]{:S(2)}) collective-permute-start(f32[256,896]{1,0:T(8,128)S(1)} %dynamic-slice_add_fusion.1), channel_id=1, source_target_pairs={{0,2},{1,3},{2,0},{3,1},{4,6},{5,7},{6,4},{7,5},{8,10},{9,11},{10,... | collective-permute-start | bytes 2752520 | tf_op jit(solution)/shard_map/ppermute | solution.py:45
  226.1 4.1 %collective-permute-start.3 = (f32[512,896]{1,0:T(8,128)}, f32[512,896]{1,0:T(8,128)}, u32[]{:S(2)}, u32[]{:S(2)}) collective-permute-start(f32[512,896]{1,0:T(8,128)} %pad_maximum_fusion.1), channel_id=1, source_target_pairs={{0,1},{1,0},{2,3},{3,2},{4,5},{5,4},{6,7},{7,6},{8,9},{9,8},{10,11... | collective-permute-start | bytes 5505032 | tf_op jit(solution)/shard_map/ppermute | solution.py:45
  233.8 4.8 %copy-start.10 = (bf16[2048,896]{1,0:T(8,128)(2,1)S(1)}, bf16[2048,896]{1,0:T(8,128)(2,1)}, u32[]{:S(2)}) copy-start(bf16[2048,896]{1,0:T(8,128)(2,1)} %param.11) | copy-start | bytes 11010052
  238.7 6.7 %copy-start.6 = (bf16[1024,896]{1,0:T(8,128)(2,1)}, bf16[1024,896]{1,0:T(8,128)(2,1)S(1)}, u32[]{:S(2)}) copy-start(bf16[1024,896]{1,0:T(8,128)(2,1)S(1)} %fusion.10) | copy-start | bytes 5505028
  238.7 6.7 %copy-start = (f32[512,896]{1,0:T(8,128)S(1)}, f32[512,896]{1,0:T(8,128)}, u32[]{:S(2)}) copy-start(f32[512,896]{1,0:T(8,128)} %get-tuple-element.4) | copy-start | bytes 5505028
  238.7 6.7 %copy-start.1 = (f32[512,896]{1,0:T(8,128)S(1)}, f32[512,896]{1,0:T(8,128)}, u32[]{:S(2)}) copy-start(f32[512,896]{1,0:T(8,128)} %get-tuple-element.5) | copy-start | bytes 5505028
  238.7 6.7 %copy-start.3 = (bf16[1024,1792]{1,0:T(8,128)(2,1)S(1)}, bf16[1024,1792]{1,0:T(8,128)(2,1)}, u32[]{:S(2)}) copy-start(bf16[1024,1792]{1,0:T(8,128)(2,1)} %all-gather.2.cloned.1.call-done) | copy-start | bytes 11010052
  255.4 73.6 %all-to-all-start.1 = ((bf16[32,32,2048]{2,1,0:T(8,128)(2,1)}), bf16[32,32,2048]{2,1,0:T(8,128)(2,1)}, u32[]{:S(2)}, u32[]{:S(2)}) async-start(bf16[32,32,2048]{2,1,0:T(8,128)(2,1)} %bitcast.7), calls=%async_computation.1 | async-start | bytes 8388608 | tf_op jit(solution)/shard_map/all_to_all | solution.py:38
  271.5 9.5 %copy-start.7 = (bf16[1024,896]{1,0:T(8,128)(2,1)S(1)}, bf16[1024,896]{1,0:T(8,128)(2,1)}, u32[]{:S(2)}) copy-start(bf16[1024,896]{1,0:T(8,128)(2,1)} %copy-done.6) | copy-start | bytes 5505028
  281.0 8.3 %copy-start.2 = (f32[512,896]{1,0:T(8,128)S(1)}, f32[512,896]{1,0:T(8,128)}, u32[]{:S(2)}) copy-start(f32[512,896]{1,0:T(8,128)} %get-tuple-element.5) | copy-start | bytes 5505028
  281.0 8.3 %copy-start.4 = (bf16[1024,1792]{1,0:T(8,128)(2,1)S(1)}, bf16[1024,1792]{1,0:T(8,128)(2,1)}, u32[]{:S(2)}) copy-start(bf16[1024,1792]{1,0:T(8,128)(2,1)} %all-gather.2.cloned.1.call-done) | copy-start | bytes 11010052
Sparse Core Ops, SparseCore 0:
  155.9 57.6 all-gather.1

commit v2 on v1

--- a/solution.py
+++ b/solution.py
@@ -70,9 +70,7 @@
 
 def make_body(rows, cols):
     def body(inputs, out_grad, gate_pre, up_pre, gate_weight, up_weight, down_weight):
-      features = out_grad.shape[1]
-      both_rows = gather_rows(jnp.concatenate([out_grad, inputs], axis=1), "row", rows)
-      grad_rows, input_rows = both_rows[:, :features], both_rows[:, features:]
+      grad_rows = gather_rows(out_grad, "row", rows)
       width = gate_pre.shape[1]
       pre_all = lax.all_gather(
           jnp.concatenate([gate_pre, up_pre], axis=1), "col", axis=0, tiled=True
@@ -82,6 +80,7 @@
       hidden_total = sum_all(partial_hidden, "col", cols)
       hidden, gate_grad, up_grad = swiglu_back(hidden_total, gate_all, up_all)
       grad_down = contract_first(hidden, grad_rows).astype(jnp.bfloat16)
+      input_rows = lax.all_gather(inputs, "row", axis=0, tiled=True)
       gate_total = contract_first(input_rows, gate_grad)
       up_total = contract_first(input_rows, up_grad)
       input_total = scatter_sum_rows(

time: 340 us -> 361 us (1.062)
  waiting for transfers between devices: 217 us -> 233 us
  local copies, waits for them, and re-layouts: 7.27 us -> 17.5 us
  starting transfers between devices: 30.9 us -> 22.5 us
    all_gather x0 -> x1, waiting for transfers between devices: none -> 112 us  [body(): input_rows = lax.all_gather(inputs, 'row', axis=0, tiled=True)]
    all_to_all x1, waiting for transfers between devices: 122 us -> 66.3 us  [gather_rows(): return lax.all_to_all(tiled, axis, 0, 0, tiled=True)]
    all_to_all x1, waiting for transfers between devices: 31.3 us -> 0.01 us  [scatter_sum_rows(): lax.all_to_all(partial.astype(jnp.bfloat16), axis, 0, 0, tiled=True)]
    unnamed x22 -> x18, local copies, waits for them, and re-layouts: 2.81 us -> 14 us
    ppermute x4, waiting for transfers between devices: 63.1 us -> 54.5 us  [swap(): return lax.ppermute(value, axis, pairs)]
    all_to_all x1, starting transfers between devices: 16.1 us -> 8.2 us  [scatter_sum_rows(): lax.all_to_all(partial.astype(jnp.bfloat16), axis, 0, 0, tiled=True)]
  transfers between devices with their start and end apart: 7 -> 8, of which waited for: 6 -> 6; matrix products, arithmetic and copies ran while one was open for 11% -> 22% of each run, Pallas kernels for 0% -> 0%
where the time goes in v2:
time: 361 us; the launch traced here: 358 us
  waiting for transfers between devices  233 us (65%)
  matrix products  51.5 us (14%)
  starting transfers between devices  22.5 us (6%)
  other arithmetic  19.3 us (5%)
  local copies, waits for them, and re-layouts  17.5 us (5%)
  between operations  14.2 us (4%)
    all_gather x1, waiting for transfers between devices, body(): input_rows = lax.all_gather(inputs, 'row', axis=0, tiled=True)  112 us
    all_to_all x1, waiting for transfers between devices, gather_rows(): return lax.all_to_all(tiled, axis, 0, 0, tiled=True)  66.3 us
    ppermute x4, waiting for transfers between devices, swap(): return lax.ppermute(value, axis, pairs)  54.5 us
    dot_general x3, matrix products, contract_first(): lax.dot_general(left, right, (((0,), (0,)), ((), ())), preferred_element_...  27.3 us
    dot_general x3, matrix products, contract_last(): lax.dot_general(left, right, (((1,), (1,)), ((), ())), preferred_element_...  24.2 us
    unnamed x18, local copies, waits for them, and re-layouts  14 us
    all_to_all x1, starting transfers between devices, gather_rows(): return lax.all_to_all(tiled, axis, 0, 0, tiled=True)  9.76 us
    all_to_all x1, starting transfers between devices, scatter_sum_rows(): lax.all_to_all(partial.astype(jnp.bfloat16), axis, 0, 0, tiled=True)  8.2 us
  transfers between devices with their start and end apart: 8, of which 6 were waited for; matrix products, arithmetic and copies ran while one was open for 22% of the time, Pallas kernels for 0%

profile of v2, /device:TPU:2, one launch (start us, length us, event | category | flops | bytes accessed | tf_op | source)
XLA Modules:
  0.0 357.7 jit_solution(1025715258002052524)
XLA Ops:
  7.2 3.4 tile.2
  10.5 0.0 copy-start.5
  10.5 0.0 copy-start.6
  10.5 9.8 %all-to-all-start = ((bf16[32,32,2048]{2,1,0:T(8,128)(2,1)}), bf16[32,32,2048]{2,1,0:T(8,128)(2,1)}, u32[]{:S(2)}, u32[]{:S(2)}) async-start(bf16[32,32,2048]{2,1,0:T(8,128)(2,1)} %tile.2), calls=%async_computation | async-start | bytes 8388608 | tf_op jit(solution)/shard_map/all_to_all | solution.py:34
  20.3 0.0 all-gather.3.cloned.1.call-start
  20.4 0.0 copy-done.5
  20.4 0.0 copy-done.6
  20.4 1.0 pad_maximum_fusion.2
  21.4 0.0 all-gather.3.cloned.1.call-update
  21.4 0.0 all-gather.5.cloned.1.call-start
  21.5 66.3 %all-to-all-done = bf16[32,32,2048]{2,1,0:T(8,128)(2,1)} async-done(((bf16[32,32,2048]{2,1,0:T(8,128)(2,1)}), bf16[32,32,2048]{2,1,0:T(8,128)(2,1)}, u32[]{:S(2)}, u32[]{:S(2)}) %all-to-all-start) | async-done | bytes 4194336 | tf_op jit(solution)/shard_map/all_to_all | solution.py:34
  87.8 7.4 %fusion.11 = f32[1024,896]{1,0:T(8,128)S(1)} fusion(bf16[1024,2048]{1,0:T(8,128)(2,1)} %bitcast, bf16[896,2048]{1,0:T(8,128)(2,1)} %param.13), kind=kOutput, calls=%fused_computation.31 | convolution fusion | flops 3758096384 | bytes 11534336 | tf_op jit(solution)/shard_map/dot_general | solution.py:21
  95.2 0.0 copy-start.3
  95.2 1.8 copy-done.3
  97.0 0.1 constant_dynamic-slice_fusion.1
  97.2 0.1 collective-permute-start
  97.3 3.9 %collective-permute-done = f32[512,896]{1,0:T(8,128)} collective-permute-done((f32[512,896]{1,0:T(8,128)S(1)}, f32[512,896]{1,0:T(8,128)}, u32[]{:S(2)}, u32[]{:S(2)}) %collective-permute-start) | collective-permute-done | bytes 1835040 | tf_op jit(solution)/shard_map/ppermute | solution.py:45
  101.2 2.2 dynamic-slice_add_fusion
  103.4 0.1 constant_dynamic-slice_fusion
  103.5 2.2 collective-permute-start.1
  105.7 21.9 %collective-permute-done.1 = f32[256,896]{1,0:T(8,128)} collective-permute-done((f32[256,896]{1,0:T(8,128)S(1)}, f32[256,896]{1,0:T(8,128)}, u32[]{:S(2)}, u32[]{:S(2)}) %collective-permute-start.1) | collective-permute-done | bytes 917536 | tf_op jit(solution)/shard_map/ppermute | solution.py:45
  127.6 1.3 dynamic-slice_add_fusion.1
  128.8 2.2 collective-permute-start.2
  131.0 0.0 all-gather.5.cloned.1.call-update
  131.1 24.7 %collective-permute-done.2 = f32[256,896]{1,0:T(8,128)} collective-permute-done((f32[256,896]{1,0:T(8,128)S(1)}, f32[256,896]{1,0:T(8,128)}, u32[]{:S(2)}, u32[]{:S(2)}) %collective-permute-start.2) | collective-permute-done | bytes 917536 | tf_op jit(solution)/shard_map/ppermute | solution.py:45
  155.7 1.3 broadcast_select_fusion.3
  157.0 1.3 pad_maximum_fusion.1
  158.4 0.0 collective-permute-start.3
  158.4 4.1 %collective-permute-done.3 = f32[512,896]{1,0:T(8,128)} collective-permute-done((f32[512,896]{1,0:T(8,128)}, f32[512,896]{1,0:T(8,128)}, u32[]{:S(2)}, u32[]{:S(2)}) %collective-permute-start.3) | collective-permute-done | bytes 1835040 | tf_op jit(solution)/shard_map/ppermute | solution.py:45
  162.5 3.7 %broadcast_select_fusion.1 = (f32[512,896]{1,0:T(8,128)}, f32[512,896]{1,0:T(8,128)}) fusion(f32[512,896]{1,0:T(8,128)} %collective-permute-done.3, pred[]{:T(512)S(6)} %eq.11, f32[256,896]{1,0:T(8,128)S(1)} %get-tuple-element.11, f32[256,896]{1,0:T(8,128)S(1)} %get-tuple-element.10), kind=kLoop, calls=%fused_computation.25 | loop fusion | flops 1376256 | bytes 7340033 | tf_op jit(solution)/shard_map/jit(_where)/select_n | solution.py:57
  166.2 0.0 all-gather.3.cloned.1.call-done
  166.2 0.0 copy-start.7
  166.2 4.8 %fusion.2 = bf16[1024,896]{1,0:T(8,128)(2,1)S(1)} fusion(f32[512,896]{1,0:T(8,128)} %get-tuple-element.9, f32[512,896]{1,0:T(8,128)} %get-tuple-element.8, bf16[1024,1792]{1,0:T(8,128)(2,1)} %all-gather.3.cloned.1.call-done), kind=kLoop, calls=%fused_computation.8 | loop fusion | flops 11927552 | bytes 9175040 | tf_op jit(solution)/shard_map/convert_element_type | solution.py:15
  171.0 0.0 copy-done.7
  171.0 0.0 copy-start.4
  171.1 0.0 copy-start
  171.1 0.0 copy-start.1
  171.1 0.0 copy-start.2
  171.1 6.7 %fusion.12 = f32[1024,2048]{1,0:T(8,128)} fusion(bf16[1024,896]{1,0:T(8,128)(2,1)S(1)} %fusion.2, bf16[2048,896]{1,0:T(8,128)(2,1)S(1)} %copy-done.7), kind=kOutput, calls=%fused_computation.32 | convolution fusion | flops 3758096384 | bytes 13893632 | tf_op jit(solution)/shard_map/dot_general | solution.py:21
  177.8 0.0 copy-done.4
  177.8 0.0 copy-done
  177.8 0.0 copy-done.1
  177.8 0.0 copy-done.2
  177.9 10.0 %add_convert_fusion = bf16[1024,2048]{1,0:T(8,128)(2,1)} fusion(f32[1024,2048]{1,0:T(8,128)} %fusion.12, bf16[2048,896]{1,0:T(8,128)(2,1)} %param.12, f32[512,896]{1,0:T(8,128)S(1)} %copy-done.1, f32[512,896]{1,0:T(8,128)S(1)} %copy-done, bf16[1024,1792]{1,0:T(8,128)(2,1)S(1)} %copy-done.2), kind=kOutput, calls=%fused_computation | convolution fusion | flops 3769630720 | bytes 21757952 | tf_op jit(solution)/shard_map/dot_general | solution.py:21
  187.9 8.2 %all-to-all-start.1 = ((bf16[32,32,2048]{2,1,0:T(8,128)(2,1)}), bf16[32,32,2048]{2,1,0:T(8,128)(2,1)}, u32[]{:S(2)}, u32[]{:S(2)}) async-start(bf16[32,32,2048]{2,1,0:T(8,128)(2,1)} %bitcast.15), calls=%async_computation.1 | async-start | bytes 8388608 | tf_op jit(solution)/shard_map/all_to_all | solution.py:38
  196.1 9.4 %convolution_convert_fusion = bf16[896,2048]{1,0:T(8,128)(2,1)} fusion(bf16[1024,2048]{1,0:T(8,128)(2,1)} %bitcast, bf16[1024,1792]{1,0:T(8,128)(2,1)} %all-gather.3.cloned.1.call-done), kind=kOutput, calls=%fused_computation.18 | convolution fusion | flops 3767271424 | bytes 11534336 | tf_op jit(solution)/shard_map/dot_general | solution.py:27
  205.5 111.8 %all-gather.5.cloned.1.call-done = bf16[1024,2048]{1,0:T(8,128)(2,1)} async-done(((bf16[32,2048]{1,0:T(8,128)(2,1)}), bf16[1024,2048]{1,0:T(8,128)(2,1)}) %all-gather.5.cloned.1.call-update) | async-done | bytes 4194320 | tf_op jit(solution)/shard_map/all_gather | solution.py:83
  317.3 8.6 %convert_bitcast_fusion.1 = bf16[2048,896]{0,1:T(8,128)(2,1)} fusion(bf16[1024,896]{1,0:T(8,128)(2,1)} %copy-done.4, bf16[1024,2048]{1,0:T(8,128)(2,1)} %all-gather.5.cloned.1.call-done), kind=kOutput, calls=%fused_computation.16 | convolution fusion | flops 3759931392 | bytes 9699328 | tf_op jit(solution)/shard_map/dot_general | solution.py:27
  325.9 6.0 %copy.11 = bf16[2048,896]{1,0:T(8,128)(2,1)} copy(bf16[2048,896]{0,1:T(8,128)(2,1)} %convert_bitcast_fusion.1) | data formatting | bytes 7340032
  331.9 9.3 %convert_bitcast_fusion = bf16[2048,896]{0,1:T(8,128)(2,1)} fusion(bf16[1024,2048]{1,0:T(8,128)(2,1)} %all-gather.5.cloned.1.call-done, f32[512,896]{1,0:T(8,128)} %get-tuple-element.9, f32[512,896]{1,0:T(8,128)S(1)} %copy-done, bf16[1024,1792]{1,0:T(8,128)(2,1)} %all-gather.3.cloned.1.call-done), kind=kOutput, calls=%fused_computation.15 | convolution fusion | flops 3767271424 | bytes 13369344 | tf_op jit(solution)/shard_map/dot_general | solution.py:27
  341.2 6.0 %copy.12 = bf16[2048,896]{1,0:T(8,128)(2,1)} copy(bf16[2048,896]{0,1:T(8,128)(2,1)} %convert_bitcast_fusion) | data formatting | bytes 7340032
  347.2 0.0 all-to-all-done.1
  347.2 3.7 %reduce_sum.12 = bf16[32,2048]{1,0:T(8,128)(2,1)} reduce(bf16[32,32,2048]{2,1,0:T(8,128)(2,1)} %all-to-all-done.1, bf16[]{:T(256)} %constant.44.clone.1), dimensions={0}, to_apply=%region_0.1 | reduce | flops 2031616 | bytes 4325378 | tf_op jit(solution)/shard_map/reduce_sum | solution.py:40
Async XLA Ops:
  10.5 9.8 %copy-start.5 = (bf16[256,896]{1,0:T(8,128)(2,1)S(1)}, bf16[256,896]{1,0:T(8,128)(2,1)}, u32[]{:S(2)}) copy-start(bf16[256,896]{1,0:T(8,128)(2,1)} %param.10) | copy-start | bytes 1376260
  10.5 9.8 %copy-start.6 = (bf16[256,896]{1,0:T(8,128)(2,1)S(1)}, bf16[256,896]{1,0:T(8,128)(2,1)}, u32[]{:S(2)}) copy-start(bf16[256,896]{1,0:T(8,128)(2,1)} %param.9) | copy-start | bytes 1376260
  10.5 77.2 %all-to-all-start = ((bf16[32,32,2048]{2,1,0:T(8,128)(2,1)}), bf16[32,32,2048]{2,1,0:T(8,128)(2,1)}, u32[]{:S(2)}, u32[]{:S(2)}) async-start(bf16[32,32,2048]{2,1,0:T(8,128)(2,1)} %tile.2), calls=%async_computation | async-start | bytes 8388608 | tf_op jit(solution)/shard_map/all_to_all | solution.py:34
  20.3 145.9 %all-gather.3.cloned.1.call-start = ((), (), s32[]{:S(2)}) async-start(), calls=%async_computation.2 | async-start | bytes 4587520 | tf_op jit(solution)/shard_map/all_gather | solution.py:75
  21.4 295.9 %all-gather.5.cloned.1.call-start = ((), (), s32[]{:S(2)}) async-start(), calls=%async_computation.3 | async-start | bytes 4325376 | tf_op jit(solution)/shard_map/all_gather | solution.py:83
  95.2 1.8 copy-start.3
  97.2 4.0 %collective-permute-start = (f32[512,896]{1,0:T(8,128)S(1)}, f32[512,896]{1,0:T(8,128)}, u32[]{:S(2)}, u32[]{:S(2)}) collective-permute-start(f32[512,896]{1,0:T(8,128)S(1)} %constant_dynamic-slice_fusion.1), channel_id=1, source_target_pairs={{0,1},{1,0},{2,3},{3,2},{4,5},{5,4},{6,7},{7,6},{8,9},{9,8},{10,11... | collective-permute-start | bytes 5505032 | tf_op jit(solution)/shard_map/ppermute | solution.py:45
  103.5 24.1 %collective-permute-start.1 = (f32[256,896]{1,0:T(8,128)S(1)}, f32[256,896]{1,0:T(8,128)}, u32[]{:S(2)}, u32[]{:S(2)}) collective-permute-start(f32[256,896]{1,0:T(8,128)S(1)} %constant_dynamic-slice_fusion), channel_id=1, source_target_pairs={{0,2},{1,3},{2,0},{3,1},{4,6},{5,7},{6,4},{7,5},{8,10},{9,11},{10,... | collective-permute-start | bytes 2752520 | tf_op jit(solution)/shard_map/ppermute | solution.py:45
  128.8 26.9 %collective-permute-start.2 = (f32[256,896]{1,0:T(8,128)S(1)}, f32[256,896]{1,0:T(8,128)}, u32[]{:S(2)}, u32[]{:S(2)}) collective-permute-start(f32[256,896]{1,0:T(8,128)S(1)} %dynamic-slice_add_fusion.1), channel_id=1, source_target_pairs={{0,2},{1,3},{2,0},{3,1},{4,6},{5,7},{6,4},{7,5},{8,10},{9,11},{10,... | collective-permute-start | bytes 2752520 | tf_op jit(solution)/shard_map/ppermute | solution.py:45
  158.4 4.1 %collective-permute-start.3 = (f32[512,896]{1,0:T(8,128)}, f32[512,896]{1,0:T(8,128)}, u32[]{:S(2)}, u32[]{:S(2)}) collective-permute-start(f32[512,896]{1,0:T(8,128)} %pad_maximum_fusion.1), channel_id=1, source_target_pairs={{0,1},{1,0},{2,3},{3,2},{4,5},{5,4},{6,7},{7,6},{8,9},{9,8},{10,11... | collective-permute-start | bytes 5505032 | tf_op jit(solution)/shard_map/ppermute | solution.py:45
  166.2 4.8 %copy-start.7 = (bf16[2048,896]{1,0:T(8,128)(2,1)S(1)}, bf16[2048,896]{1,0:T(8,128)(2,1)}, u32[]{:S(2)}) copy-start(bf16[2048,896]{1,0:T(8,128)(2,1)} %param.11) | copy-start | bytes 11010052
  171.0 6.8 %copy-start.4 = (bf16[1024,896]{1,0:T(8,128)(2,1)}, bf16[1024,896]{1,0:T(8,128)(2,1)S(1)}, u32[]{:S(2)}) copy-start(bf16[1024,896]{1,0:T(8,128)(2,1)S(1)} %fusion.2) | copy-start | bytes 5505028
  171.1 6.8 %copy-start = (f32[512,896]{1,0:T(8,128)S(1)}, f32[512,896]{1,0:T(8,128)}, u32[]{:S(2)}) copy-start(f32[512,896]{1,0:T(8,128)} %get-tuple-element.8) | copy-start | bytes 5505028
  171.1 6.8 %copy-start.1 = (f32[512,896]{1,0:T(8,128)S(1)}, f32[512,896]{1,0:T(8,128)}, u32[]{:S(2)}) copy-start(f32[512,896]{1,0:T(8,128)} %get-tuple-element.9) | copy-start | bytes 5505028
  171.1 6.8 %copy-start.2 = (bf16[1024,1792]{1,0:T(8,128)(2,1)S(1)}, bf16[1024,1792]{1,0:T(8,128)(2,1)}, u32[]{:S(2)}) copy-start(bf16[1024,1792]{1,0:T(8,128)(2,1)} %all-gather.3.cloned.1.call-done) | copy-start | bytes 11010052
  187.9 159.3 %all-to-all-start.1 = ((bf16[32,32,2048]{2,1,0:T(8,128)(2,1)}), bf16[32,32,2048]{2,1,0:T(8,128)(2,1)}, u32[]{:S(2)}, u32[]{:S(2)}) async-start(bf16[32,32,2048]{2,1,0:T(8,128)(2,1)} %bitcast.15), calls=%async_computation.1 | async-start | bytes 8388608 | tf_op jit(solution)/shard_map/all_to_all | solution.py:38
Sparse Core Ops, SparseCore 0:
  23.4 55.1 all-gather.2
  131.2 186.0 all-gather.4

commit v3 on v2

--- a/solution.py
+++ b/solution.py
@@ -40,20 +40,21 @@
     return received.astype(jnp.float32).sum(0)
 
 
-def swap(value, axis, count, bit):
+def swap(value, axis, count, bit, pieces=1):
     pairs = [(i, i ^ bit) for i in range(count)]
-    return lax.ppermute(value, axis, pairs)
+    parts = jnp.split(value, pieces, axis=0)
+    return jnp.concatenate([lax.ppermute(part, axis, pairs) for part in parts], axis=0)
 
 
-def halve_sum(value, axis, count, bit, own):
+def halve_sum(value, axis, count, bit, own, pieces=1):
     half = value.shape[0] // 2
     keep = lax.dynamic_slice_in_dim(value, own * half, half, axis=0)
     give = lax.dynamic_slice_in_dim(value, (1 - own) * half, half, axis=0)
-    return keep + swap(give, axis, count, bit)
+    return keep + swap(give, axis, count, bit, pieces)
 
 
-def double(value, axis, count, bit, own):
-    other = swap(value, axis, count, bit)
+def double(value, axis, count, bit, own, pieces=1):
+    other = swap(value, axis, count, bit, pieces)
     first = jnp.where(own == 0, value, other)
     second = jnp.where(own == 0, other, value)
     return jnp.concatenate([first, second], axis=0)
@@ -63,8 +64,8 @@
     index = lax.axis_index(axis)
     near, far = index % 2, (index // 2) % 2
     total = halve_sum(partial, axis, count, 1, near)
-    total = halve_sum(total, axis, count, 2, far)
-    total = double(total, axis, count, 2, far)
+    total = halve_sum(total, axis, count, 2, far, 4)
+    total = double(total, axis, count, 2, far, 4)
     return double(total, axis, count, 1, near)
 
 

time: 361 us -> 364 us (level)
  starting transfers between devices: 22.5 us -> 33.5 us
  waiting for transfers between devices: 233 us -> 228 us
    ppermute x4 -> x10, waiting for transfers between devices: 54.5 us -> 42.1 us  [swap(): lax.ppermute(part, axis, pairs)]
    ppermute x4 -> x10, starting transfers between devices: 4.5 us -> 14.4 us  [swap(): lax.ppermute(part, axis, pairs)]
    all_gather x1, waiting for transfers between devices: 112 us -> 119 us  [body(): input_rows = lax.all_gather(inputs, 'row', axis=0, tiled=True)]
    unnamed x18 -> x21, local copies, waits for them, and re-layouts: 14 us -> 14 us
  transfers between devices with their start and end apart: 8 -> 14, of which waited for: 6 -> 12; matrix products, arithmetic and copies ran while one was open for 22% -> 22% of each run, Pallas kernels for 0% -> 0%
where the time goes in v3:
time: 364 us; the launch traced here: 363 us
  waiting for transfers between devices  228 us (63%)
  matrix products  51.5 us (14%)
  starting transfers between devices  33.5 us (9%)
  other arithmetic  18 us (5%)
  local copies, waits for them, and re-layouts  17.7 us (5%)
  between operations  14.3 us (4%)
    all_gather x1, waiting for transfers between devices, body(): input_rows = lax.all_gather(inputs, 'row', axis=0, tiled=True)  119 us
    all_to_all x1, waiting for transfers between devices, gather_rows(): return lax.all_to_all(tiled, axis, 0, 0, tiled=True)  66.3 us
    ppermute x10, waiting for transfers between devices, swap(): lax.ppermute(part, axis, pairs)  42.1 us
    dot_general x3, matrix products, contract_first(): lax.dot_general(left, right, (((0,), (0,)), ((), ())), preferred_element_...  27.3 us
    dot_general x3, matrix products, contract_last(): lax.dot_general(left, right, (((1,), (1,)), ((), ())), preferred_element_...  24.2 us
    ppermute x10, starting transfers between devices, swap(): lax.ppermute(part, axis, pairs)  14.4 us
    unnamed x21, local copies, waits for them, and re-layouts  14 us
    all_to_all x1, starting transfers between devices, gather_rows(): return lax.all_to_all(tiled, axis, 0, 0, tiled=True)  9.76 us
  transfers between devices with their start and end apart: 14, of which 12 were waited for; matrix products, arithmetic and copies ran while one was open for 22% of the time, Pallas kernels for 0%

profile of v3, /device:TPU:2, one launch (start us, length us, event | category | flops | bytes accessed | tf_op | source)
XLA Modules:
  0.0 362.5 jit_solution(14051232660112253863)
XLA Ops:
  7.2 3.4 tile.2
  10.6 0.0 copy-start.5
  10.6 0.0 copy-start.6
  10.6 9.8 %all-to-all-start = ((bf16[32,32,2048]{2,1,0:T(8,128)(2,1)}), bf16[32,32,2048]{2,1,0:T(8,128)(2,1)}, u32[]{:S(2)}, u32[]{:S(2)}) async-start(bf16[32,32,2048]{2,1,0:T(8,128)(2,1)} %tile.2), calls=%async_computation | async-start | bytes 8388608 | tf_op jit(solution)/shard_map/all_to_all | solution.py:34
  20.3 0.0 all-gather.3.cloned.1.call-start
  20.4 0.0 copy-done.5
  20.4 0.0 copy-done.6
  20.4 1.0 pad_maximum_fusion.2
  21.4 0.0 all-gather.3.cloned.1.call-update
  21.4 0.0 all-gather.5.cloned.1.call-start
  21.5 66.3 %all-to-all-done = bf16[32,32,2048]{2,1,0:T(8,128)(2,1)} async-done(((bf16[32,32,2048]{2,1,0:T(8,128)(2,1)}), bf16[32,32,2048]{2,1,0:T(8,128)(2,1)}, u32[]{:S(2)}, u32[]{:S(2)}) %all-to-all-start) | async-done | bytes 4194336 | tf_op jit(solution)/shard_map/all_to_all | solution.py:34
  87.8 7.4 %fusion.12 = f32[1024,896]{1,0:T(8,128)S(1)} fusion(bf16[1024,2048]{1,0:T(8,128)(2,1)} %bitcast, bf16[896,2048]{1,0:T(8,128)(2,1)} %param.13), kind=kOutput, calls=%fused_computation.39 | convolution fusion | flops 3758096384 | bytes 11534336 | tf_op jit(solution)/shard_map/dot_general | solution.py:21
  95.2 0.0 copy-start.3
  95.2 1.8 copy-done.3
  97.1 0.1 constant_dynamic-slice_fusion.4
  97.2 0.1 collective-permute-start
  97.3 3.9 %collective-permute-done = f32[512,896]{1,0:T(8,128)} collective-permute-done((f32[512,896]{1,0:T(8,128)S(1)}, f32[512,896]{1,0:T(8,128)}, u32[]{:S(2)}, u32[]{:S(2)}) %collective-permute-start) | collective-permute-done | bytes 1835040 | tf_op jit(solution)/shard_map/ppermute | solution.py:46
  101.2 2.2 dynamic-slice_add_fusion
  103.4 0.1 constant_dynamic-slice_fusion.2
  103.5 2.2 collective-permute-start.4
  105.7 1.4 collective-permute-start.3
  107.1 2.1 collective-permute-start.2
  109.2 1.4 collective-permute-start.1
  110.6 2.9 collective-permute-done.4
  113.5 4.9 %collective-permute-done.3 = f32[64,896]{1,0:T(8,128)S(1)} collective-permute-done((f32[64,896]{1,0:T(8,128)S(1)}, f32[64,896]{1,0:T(8,128)S(1)}, u32[]{:S(2)}, u32[]{:S(2)}) %collective-permute-start.3) | collective-permute-done | bytes 229408 | tf_op jit(solution)/shard_map/ppermute | solution.py:46
  118.5 4.9 %collective-permute-done.2 = f32[64,896]{1,0:T(8,128)S(1)} collective-permute-done((f32[64,896]{1,0:T(8,128)S(1)}, f32[64,896]{1,0:T(8,128)S(1)}, u32[]{:S(2)}, u32[]{:S(2)}) %collective-permute-start.2) | collective-permute-done | bytes 229408 | tf_op jit(solution)/shard_map/ppermute | solution.py:46
  123.4 4.2 %collective-permute-done.1 = f32[64,896]{1,0:T(8,128)} collective-permute-done((f32[64,896]{1,0:T(8,128)S(1)}, f32[64,896]{1,0:T(8,128)}, u32[]{:S(2)}, u32[]{:S(2)}) %collective-permute-start.1) | collective-permute-done | bytes 229408 | tf_op jit(solution)/shard_map/ppermute | solution.py:46
  127.6 1.0 maximum_add_fusion
  128.6 0.1 fusion.11
  128.7 2.2 collective-permute-start.5
  130.9 1.4 collective-permute-start.6
  132.3 0.0 all-gather.5.cloned.1.call-update
  132.3 2.2 collective-permute-start.7
  134.5 1.4 collective-permute-start.8
  135.9 2.8 collective-permute-done.5
  138.8 4.9 %collective-permute-done.6 = f32[64,896]{1,0:T(8,128)S(1)} collective-permute-done((f32[64,896]{1,0:T(8,128)S(1)}, f32[64,896]{1,0:T(8,128)S(1)}, u32[]{:S(2)}, u32[]{:S(2)}) %collective-permute-start.6) | collective-permute-done | bytes 229408 | tf_op jit(solution)/shard_map/ppermute | solution.py:46
  143.7 6.3 %collective-permute-done.7 = f32[64,896]{1,0:T(8,128)S(1)} collective-permute-done((f32[64,896]{1,0:T(8,128)S(1)}, f32[64,896]{1,0:T(8,128)S(1)}, u32[]{:S(2)}, u32[]{:S(2)}) %collective-permute-start.7) | collective-permute-done | bytes 229408 | tf_op jit(solution)/shard_map/ppermute | solution.py:46
  150.0 3.2 collective-permute-done.8
  153.2 0.2 broadcast_select_fusion.3
  153.5 1.3 pad_maximum_fusion.1
  154.8 0.0 collective-permute-start.9
  154.8 4.1 %collective-permute-done.9 = f32[512,896]{1,0:T(8,128)} collective-permute-done((f32[512,896]{1,0:T(8,128)}, f32[512,896]{1,0:T(8,128)}, u32[]{:S(2)}, u32[]{:S(2)}) %collective-permute-start.9) | collective-permute-done | bytes 1835040 | tf_op jit(solution)/shard_map/ppermute | solution.py:46
  158.9 3.6 %broadcast_select_fusion.1 = (f32[512,896]{1,0:T(8,128)}, f32[512,896]{1,0:T(8,128)}) fusion(f32[512,896]{1,0:T(8,128)} %collective-permute-done.9, pred[]{:T(512)S(6)} %eq.11, f32[256,896]{1,0:T(8,128)S(1)} %get-tuple-element.11, f32[256,896]{1,0:T(8,128)S(1)} %get-tuple-element.10), kind=kLoop, calls=%fused_computation.25 | loop fusion | flops 1376256 | bytes 7340033 | tf_op jit(solution)/shard_map/jit(_where)/select_n | solution.py:58
  162.6 4.9 %fusion.2 = bf16[1024,896]{1,0:T(8,128)(2,1)S(1)} fusion(f32[512,896]{1,0:T(8,128)} %get-tuple-element.9, f32[512,896]{1,0:T(8,128)} %get-tuple-element.8, bf16[1024,1792]{1,0:T(8,128)(2,1)} %all-gather.3.cloned.1.call-done), kind=kLoop, calls=%fused_computation.8 | loop fusion | flops 11927552 | bytes 9175040 | tf_op jit(solution)/shard_map/convert_element_type | solution.py:15
  167.4 0.0 copy-done.7
  167.5 0.0 copy-start.4
  167.5 0.0 copy-start
  167.5 0.0 copy-start.1
  167.5 0.0 copy-start.2
  167.5 6.7 %fusion.13 = f32[1024,2048]{1,0:T(8,128)} fusion(bf16[1024,896]{1,0:T(8,128)(2,1)S(1)} %fusion.2, bf16[2048,896]{1,0:T(8,128)(2,1)S(1)} %copy-done.7), kind=kOutput, calls=%fused_computation.40 | convolution fusion | flops 3758096384 | bytes 13893632 | tf_op jit(solution)/shard_map/dot_general | solution.py:21
  174.2 0.0 copy-done.4
  174.3 0.0 copy-done
  174.3 0.0 copy-done.1
  174.3 0.0 copy-done.2
  174.3 10.1 %add_convert_fusion = bf16[1024,2048]{1,0:T(8,128)(2,1)} fusion(f32[1024,2048]{1,0:T(8,128)} %fusion.13, bf16[2048,896]{1,0:T(8,128)(2,1)} %param.12, f32[512,896]{1,0:T(8,128)S(1)} %copy-done.1, f32[512,896]{1,0:T(8,128)S(1)} %copy-done, bf16[1024,1792]{1,0:T(8,128)(2,1)S(1)} %copy-done.2), kind=kOutput, calls=%fused_computation | convolution fusion | flops 3769630720 | bytes 21757952 | tf_op jit(solution)/shard_map/dot_general | solution.py:21
  184.3 9.2 %all-to-all-start.1 = ((bf16[32,32,2048]{2,1,0:T(8,128)(2,1)}), bf16[32,32,2048]{2,1,0:T(8,128)(2,1)}, u32[]{:S(2)}, u32[]{:S(2)}) async-start(bf16[32,32,2048]{2,1,0:T(8,128)(2,1)} %bitcast.15), calls=%async_computation.1 | async-start | bytes 8388608 | tf_op jit(solution)/shard_map/all_to_all | solution.py:38
  193.6 9.4 %convolution_convert_fusion = bf16[896,2048]{1,0:T(8,128)(2,1)} fusion(bf16[1024,2048]{1,0:T(8,128)(2,1)} %bitcast, bf16[1024,1792]{1,0:T(8,128)(2,1)} %all-gather.3.cloned.1.call-done), kind=kOutput, calls=%fused_computation.18 | convolution fusion | flops 3767271424 | bytes 11534336 | tf_op jit(solution)/shard_map/dot_general | solution.py:27
  203.0 119.0 %all-gather.5.cloned.1.call-done = bf16[1024,2048]{1,0:T(8,128)(2,1)} async-done(((bf16[32,2048]{1,0:T(8,128)(2,1)}), bf16[1024,2048]{1,0:T(8,128)(2,1)}) %all-gather.5.cloned.1.call-update) | async-done | bytes 4194320 | tf_op jit(solution)/shard_map/all_gather | solution.py:84
  322.0 8.6 %convert_bitcast_fusion.1 = bf16[2048,896]{0,1:T(8,128)(2,1)} fusion(bf16[1024,896]{1,0:T(8,128)(2,1)} %copy-done.4, bf16[1024,2048]{1,0:T(8,128)(2,1)} %all-gather.5.cloned.1.call-done), kind=kOutput, calls=%fused_computation.16 | convolution fusion | flops 3759931392 | bytes 9699328 | tf_op jit(solution)/shard_map/dot_general | solution.py:27
  330.6 6.0 %copy.11 = bf16[2048,896]{1,0:T(8,128)(2,1)} copy(bf16[2048,896]{0,1:T(8,128)(2,1)} %convert_bitcast_fusion.1) | data formatting | bytes 7340032
  336.7 9.3 %convert_bitcast_fusion = bf16[2048,896]{0,1:T(8,128)(2,1)} fusion(bf16[1024,2048]{1,0:T(8,128)(2,1)} %all-gather.5.cloned.1.call-done, f32[512,896]{1,0:T(8,128)} %get-tuple-element.9, f32[512,896]{1,0:T(8,128)S(1)} %copy-done, bf16[1024,1792]{1,0:T(8,128)(2,1)} %all-gather.3.cloned.1.call-done), kind=kOutput, calls=%fused_computation.15 | convolution fusion | flops 3767271424 | bytes 13369344 | tf_op jit(solution)/shard_map/dot_general | solution.py:27
  346.0 6.0 %copy.12 = bf16[2048,896]{1,0:T(8,128)(2,1)} copy(bf16[2048,896]{0,1:T(8,128)(2,1)} %convert_bitcast_fusion) | data formatting | bytes 7340032
  352.0 0.0 all-to-all-done.1
  352.0 3.7 %reduce_sum.12 = bf16[32,2048]{1,0:T(8,128)(2,1)} reduce(bf16[32,32,2048]{2,1,0:T(8,128)(2,1)} %all-to-all-done.1, bf16[]{:T(256)} %constant.44.clone.1), dimensions={0}, to_apply=%region_0.1 | reduce | flops 2031616 | bytes 4325378 | tf_op jit(solution)/shard_map/reduce_sum | solution.py:40
  (6 shorter events, 0.1 us)
Async XLA Ops:
  10.6 9.8 %copy-start.5 = (bf16[256,896]{1,0:T(8,128)(2,1)S(1)}, bf16[256,896]{1,0:T(8,128)(2,1)}, u32[]{:S(2)}) copy-start(bf16[256,896]{1,0:T(8,128)(2,1)} %param.10) | copy-start | bytes 1376260
  10.6 9.8 %copy-start.6 = (bf16[256,896]{1,0:T(8,128)(2,1)S(1)}, bf16[256,896]{1,0:T(8,128)(2,1)}, u32[]{:S(2)}) copy-start(bf16[256,896]{1,0:T(8,128)(2,1)} %param.9) | copy-start | bytes 1376260
  10.6 77.2 %all-to-all-start = ((bf16[32,32,2048]{2,1,0:T(8,128)(2,1)}), bf16[32,32,2048]{2,1,0:T(8,128)(2,1)}, u32[]{:S(2)}, u32[]{:S(2)}) async-start(bf16[32,32,2048]{2,1,0:T(8,128)(2,1)} %tile.2), calls=%async_computation | async-start | bytes 8388608 | tf_op jit(solution)/shard_map/all_to_all | solution.py:34
  20.3 142.3 %all-gather.3.cloned.1.call-start = ((), (), s32[]{:S(2)}) async-start(), calls=%async_computation.2 | async-start | bytes 4587520 | tf_op jit(solution)/shard_map/all_gather | solution.py:76
  21.4 300.6 %all-gather.5.cloned.1.call-start = ((), (), s32[]{:S(2)}) async-start(), calls=%async_computation.3 | async-start | bytes 4325376 | tf_op jit(solution)/shard_map/all_gather | solution.py:84
  95.2 1.8 copy-start.3
  97.2 4.0 %collective-permute-start = (f32[512,896]{1,0:T(8,128)S(1)}, f32[512,896]{1,0:T(8,128)}, u32[]{:S(2)}, u32[]{:S(2)}) collective-permute-start(f32[512,896]{1,0:T(8,128)S(1)} %constant_dynamic-slice_fusion.4), channel_id=1, source_target_pairs={{0,1},{1,0},{2,3},{3,2},{4,5},{5,4},{6,7},{7,6},{8,9},{9,8},{10,11... | collective-permute-start | bytes 5505032 | tf_op jit(solution)/shard_map/ppermute | solution.py:46
  103.5 10.1 %collective-permute-start.4 = (f32[64,896]{1,0:T(8,128)S(1)}, f32[64,896]{1,0:T(8,128)S(1)}, u32[]{:S(2)}, u32[]{:S(2)}) collective-permute-start(f32[64,896]{1,0:T(8,128)S(1)} %get-tuple-element.15), channel_id=1, source_target_pairs={{0,2},{1,3},{2,0},{3,1},{4,6},{5,7},{6,4},{7,5},{8,10},{9,11},{10,... | collective-permute-start | bytes 688136 | tf_op jit(solution)/shard_map/ppermute | solution.py:46
  105.7 12.8 %collective-permute-start.3 = (f32[64,896]{1,0:T(8,128)S(1)}, f32[64,896]{1,0:T(8,128)S(1)}, u32[]{:S(2)}, u32[]{:S(2)}) collective-permute-start(f32[64,896]{1,0:T(8,128)S(1)} %get-tuple-element.13), channel_id=1, source_target_pairs={{0,2},{1,3},{2,0},{3,1},{4,6},{5,7},{6,4},{7,5},{8,10},{9,11},{10,... | collective-permute-start | bytes 688136 | tf_op jit(solution)/shard_map/ppermute | solution.py:46
  107.1 16.3 %collective-permute-start.2 = (f32[64,896]{1,0:T(8,128)S(1)}, f32[64,896]{1,0:T(8,128)S(1)}, u32[]{:S(2)}, u32[]{:S(2)}) collective-permute-start(f32[64,896]{1,0:T(8,128)S(1)} %get-tuple-element.14), channel_id=1, source_target_pairs={{0,2},{1,3},{2,0},{3,1},{4,6},{5,7},{6,4},{7,5},{8,10},{9,11},{10,... | collective-permute-start | bytes 688136 | tf_op jit(solution)/shard_map/ppermute | solution.py:46
  109.2 18.3 %collective-permute-start.1 = (f32[64,896]{1,0:T(8,128)S(1)}, f32[64,896]{1,0:T(8,128)}, u32[]{:S(2)}, u32[]{:S(2)}) collective-permute-start(f32[64,896]{1,0:T(8,128)S(1)} %get-tuple-element.12), channel_id=1, source_target_pairs={{0,2},{1,3},{2,0},{3,1},{4,6},{5,7},{6,4},{7,5},{8,10},{9,11},{10,... | collective-permute-start | bytes 688136 | tf_op jit(solution)/shard_map/ppermute | solution.py:46
  128.7 10.1 %collective-permute-start.5 = (f32[64,896]{1,0:T(8,128)S(1)}, f32[64,896]{1,0:T(8,128)S(1)}, u32[]{:S(2)}, u32[]{:S(2)}) collective-permute-start(f32[64,896]{1,0:T(8,128)S(1)} %get-tuple-element.19), channel_id=1, source_target_pairs={{0,2},{1,3},{2,0},{3,1},{4,6},{5,7},{6,4},{7,5},{8,10},{9,11},{10,... | collective-permute-start | bytes 688136 | tf_op jit(solution)/shard_map/ppermute | solution.py:46
  130.9 12.8 %collective-permute-start.6 = (f32[64,896]{1,0:T(8,128)S(1)}, f32[64,896]{1,0:T(8,128)S(1)}, u32[]{:S(2)}, u32[]{:S(2)}) collective-permute-start(f32[64,896]{1,0:T(8,128)S(1)} %get-tuple-element.18), channel_id=1, source_target_pairs={{0,2},{1,3},{2,0},{3,1},{4,6},{5,7},{6,4},{7,5},{8,10},{9,11},{10,... | collective-permute-start | bytes 688136 | tf_op jit(solution)/shard_map/ppermute | solution.py:46
  132.3 17.7 %collective-permute-start.7 = (f32[64,896]{1,0:T(8,128)S(1)}, f32[64,896]{1,0:T(8,128)S(1)}, u32[]{:S(2)}, u32[]{:S(2)}) collective-permute-start(f32[64,896]{1,0:T(8,128)S(1)} %get-tuple-element.17), channel_id=1, source_target_pairs={{0,2},{1,3},{2,0},{3,1},{4,6},{5,7},{6,4},{7,5},{8,10},{9,11},{10,... | collective-permute-start | bytes 688136 | tf_op jit(solution)/shard_map/ppermute | solution.py:46
  134.5 18.7 %collective-permute-start.8 = (f32[64,896]{1,0:T(8,128)S(1)}, f32[64,896]{1,0:T(8,128)S(1)}, u32[]{:S(2)}, u32[]{:S(2)}) collective-permute-start(f32[64,896]{1,0:T(8,128)S(1)} %get-tuple-element.16), channel_id=1, source_target_pairs={{0,2},{1,3},{2,0},{3,1},{4,6},{5,7},{6,4},{7,5},{8,10},{9,11},{10,... | collective-permute-start | bytes 688136 | tf_op jit(solution)/shard_map/ppermute | solution.py:46
  154.8 4.1 %collective-permute-start.9 = (f32[512,896]{1,0:T(8,128)}, f32[512,896]{1,0:T(8,128)}, u32[]{:S(2)}, u32[]{:S(2)}) collective-permute-start(f32[512,896]{1,0:T(8,128)} %pad_maximum_fusion.1), channel_id=1, source_target_pairs={{0,1},{1,0},{2,3},{3,2},{4,5},{5,4},{6,7},{7,6},{8,9},{9,8},{10,11... | collective-permute-start | bytes 5505032 | tf_op jit(solution)/shard_map/ppermute | solution.py:46
  162.6 4.9 %copy-start.7 = (bf16[2048,896]{1,0:T(8,128)(2,1)S(1)}, bf16[2048,896]{1,0:T(8,128)(2,1)}, u32[]{:S(2)}) copy-start(bf16[2048,896]{1,0:T(8,128)(2,1)} %param.11) | copy-start | bytes 11010052
  167.5 6.8 %copy-start.4 = (bf16[1024,896]{1,0:T(8,128)(2,1)}, bf16[1024,896]{1,0:T(8,128)(2,1)S(1)}, u32[]{:S(2)}) copy-start(bf16[1024,896]{1,0:T(8,128)(2,1)S(1)} %fusion.2) | copy-start | bytes 5505028
  167.5 6.8 %copy-start = (f32[512,896]{1,0:T(8,128)S(1)}, f32[512,896]{1,0:T(8,128)}, u32[]{:S(2)}) copy-start(f32[512,896]{1,0:T(8,128)} %get-tuple-element.8) | copy-start | bytes 5505028
  167.5 6.8 %copy-start.1 = (f32[512,896]{1,0:T(8,128)S(1)}, f32[512,896]{1,0:T(8,128)}, u32[]{:S(2)}) copy-start(f32[512,896]{1,0:T(8,128)} %get-tuple-element.9) | copy-start | bytes 5505028
  167.5 6.8 %copy-start.2 = (bf16[1024,1792]{1,0:T(8,128)(2,1)S(1)}, bf16[1024,1792]{1,0:T(8,128)(2,1)}, u32[]{:S(2)}) copy-start(bf16[1024,1792]{1,0:T(8,128)(2,1)} %all-gather.3.cloned.1.call-done) | copy-start | bytes 11010052
  184.3 167.7 %all-to-all-start.1 = ((bf16[32,32,2048]{2,1,0:T(8,128)(2,1)}), bf16[32,32,2048]{2,1,0:T(8,128)(2,1)}, u32[]{:S(2)}, u32[]{:S(2)}) async-start(bf16[32,32,2048]{2,1,0:T(8,128)(2,1)} %bitcast.15), calls=%async_computation.1 | async-start | bytes 8388608 | tf_op jit(solution)/shard_map/all_to_all | solution.py:38
Sparse Core Ops, SparseCore 0:
  23.4 55.1 all-gather.2
  132.4 189.5 all-gather.4

commit v4 on v2

--- a/solution.py
+++ b/solution.py
@@ -1,7 +1,7 @@
 import jax
 import jax.numpy as jnp
 from jax import lax
-from jax.sharding import PartitionSpec as P
+from jax.sharding import Mesh, PartitionSpec as P
 
 
 def swiglu_back(hidden_grad, gate_stored, up_stored):
@@ -68,24 +68,30 @@
     return double(total, axis, count, 1, near)
 
 
+ROW_PARTS = ("row_a", "row_b", "row_c")
+COL_PARTS = ("col_a", "col_b")
+
+
 def make_body(rows, cols):
     def body(inputs, out_grad, gate_pre, up_pre, gate_weight, up_weight, down_weight):
-      grad_rows = gather_rows(out_grad, "row", rows)
+      grad_rows = gather_rows(out_grad, ROW_PARTS, rows)
       width = gate_pre.shape[1]
       pre_all = lax.all_gather(
-          jnp.concatenate([gate_pre, up_pre], axis=1), "col", axis=0, tiled=True
+          jnp.concatenate([gate_pre, up_pre], axis=1), COL_PARTS, axis=0, tiled=True
       )
       gate_all, up_all = pre_all[:, :width], pre_all[:, width:]
       partial_hidden = contract_last(grad_rows, down_weight)
-      hidden_total = sum_all(partial_hidden, "col", cols)
+      hidden_total = sum_all(partial_hidden, COL_PARTS, cols)
       hidden, gate_grad, up_grad = swiglu_back(hidden_total, gate_all, up_all)
       grad_down = contract_first(hidden, grad_rows).astype(jnp.bfloat16)
-      input_rows = lax.all_gather(inputs, "row", axis=0, tiled=True)
+      input_rows = inputs
+      for part in reversed(ROW_PARTS):
+          input_rows = lax.all_gather(input_rows, part, axis=0, tiled=True)
       gate_total = contract_first(input_rows, gate_grad)
       up_total = contract_first(input_rows, up_grad)
       input_total = scatter_sum_rows(
           contract_last(gate_grad, gate_weight) + contract_last(up_grad, up_weight),
-          "row",
+          ROW_PARTS,
           rows,
       )
       return (
@@ -110,4 +116,7 @@
     )
     out_specs = (P("row", "col"), P("col", "row"), P("col", "row"), P("row", "col"))
     body = make_body(mesh.shape["row"], mesh.shape["col"])
-    return jax.shard_map(body, mesh=mesh, in_specs=in_specs, out_specs=out_specs, check_vma=False)
+    fine = Mesh(mesh.devices.reshape(2, mesh.shape["row"] // 8, 4, 2, mesh.shape["col"] // 2), ROW_PARTS + COL_PARTS)
+    in_specs = tuple(P(*(ROW_PARTS if a == "row" else COL_PARTS for a in spec)) for spec in in_specs)
+    out_specs = tuple(P(*(ROW_PARTS if a == "row" else COL_PARTS for a in spec)) for spec in out_specs)
+    return jax.shard_map(body, mesh=fine, in_specs=in_specs, out_specs=out_specs, check_vma=False)

time: 361 us -> 295 us (0.82)
  waiting for transfers between devices: 233 us -> 103 us
  blocking collectives: 0 us -> 60 us
    all_gather x2 -> x3, waiting for transfers between devices: 112 us -> 38 us  [the longest x2 38 us: body(): input_rows = lax.all_gather(input_rows, part, axis=0, tiled=True)]
    all_to_all x1, waiting for transfers between devices: 66.3 us -> 0.01 us  [gather_rows(): return lax.all_to_all(tiled, axis, 0, 0, tiled=True)]
    all_gather x0 -> x1, blocking collectives: none -> 60 us  [body(): input_rows = lax.all_gather(input_rows, part, axis=0, tiled=True)]
    ppermute x4, waiting for transfers between devices: 54.5 us -> 65.4 us  [swap(): return lax.ppermute(value, axis, pairs)]
    unnamed x18 -> x20, local copies, waits for them, and re-layouts: 14 us -> 14.9 us
  transfers between devices with their start and end apart: 8 -> 9, of which waited for: 6 -> 5; matrix products, arithmetic and copies ran while one was open for 22% -> 27% of each run, Pallas kernels for 0% -> 0%
where the time goes in v4:
time: 295 us; the launch traced here: 292 us
  waiting for transfers between devices  103 us (35%)
  blocking collectives  60 us (20%)
  matrix products  52.1 us (18%)
  starting transfers between devices  25 us (8%)
  other arithmetic  19.3 us (7%)
  local copies, waits for them, and re-layouts  18.5 us (6%)
  between operations  14 us (5%)
    ppermute x4, waiting for transfers between devices, swap(): return lax.ppermute(value, axis, pairs)  65.4 us
    all_gather x1, blocking collectives, body(): input_rows = lax.all_gather(input_rows, part, axis=0, tiled=True)  60 us
    all_gather x2, waiting for transfers between devices, body(): input_rows = lax.all_gather(input_rows, part, axis=0, tiled=True)  38 us
    dot_general x3, matrix products, contract_first(): lax.dot_general(left, right, (((0,), (0,)), ((), ())), preferred_element_...  27.3 us
    dot_general x3, matrix products, contract_last(): lax.dot_general(left, right, (((1,), (1,)), ((), ())), preferred_element_...  24.8 us
    unnamed x20, local copies, waits for them, and re-layouts  14.9 us
    all_to_all x1, starting transfers between devices, scatter_sum_rows(): lax.all_to_all(partial.astype(jnp.bfloat16), axis, 0, 0, tiled=True)  10.7 us
    all_to_all x1, starting transfers between devices, gather_rows(): return lax.all_to_all(tiled, axis, 0, 0, tiled=True)  9.75 us
  transfers between devices with their start and end apart: 9, of which 5 were waited for; matrix products, arithmetic and copies ran while one was open for 27% of the time, Pallas kernels for 0%

profile of v4, /device:TPU:2, one launch (start us, length us, event | category | flops | bytes accessed | tf_op | source)
XLA Modules:
  0.0 292.4 jit_solution(1072737459105648606)
XLA Ops:
  7.2 3.4 %tile.2 = bf16[32,32,2048]{2,1,0:T(8,128)(2,1)} broadcast(bf16[32,2048]{1,0:T(8,128)(2,1)} %param.8), dimensions={1,2} | broadcast | bytes 4325376 | tf_op jit(solution)/shard_map/tile | solution.py:33
  10.5 0.0 copy-start.7
  10.5 9.8 %all-to-all-start = ((bf16[32,32,2048]{2,1,0:T(8,128)(2,1)}), bf16[32,32,2048]{2,1,0:T(8,128)(2,1)}, u32[]{:S(2)}, u32[]{:S(2)}) async-start(bf16[32,32,2048]{2,1,0:T(8,128)(2,1)} %tile.2), calls=%async_computation | async-start | bytes 8388608 | tf_op jit(solution)/shard_map/all_to_all | solution.py:34
  20.3 0.0 all-gather.6.cloned.1.call-start
  20.3 0.0 copy-done.7
  20.4 60.0 %all_gather.13 = bf16[128,2048]{1,0:T(8,128)(2,1)} all-gather(bf16[32,2048]{1,0:T(8,128)(2,1)S(1)} %copy-done.7), channel_id=1, replica_groups=mesh['row_a'=2,'row_b'=4,'row_c'=4,'col_a'=2,'col_b'=2] {'row_c'}, dimensions={0}, use_global_device_ids=true | all-gather | bytes 655360 | tf_op jit(solution)/shard_map/all_gather | solution.py:89
  80.4 0.0 all-gather.6.cloned.1.call-update
  80.4 0.0 all-gather.4.cloned.1.call-start
  80.5 0.0 all-to-all-done
  80.5 7.4 %fusion.11 = f32[1024,896]{1,0:T(8,128)S(1)} fusion(bf16[1024,2048]{1,0:T(8,128)(2,1)} %bitcast, bf16[896,2048]{1,0:T(8,128)(2,1)} %param.13), kind=kOutput, calls=%fused_computation.31 | convolution fusion | flops 3758096384 | bytes 11534336 | tf_op jit(solution)/shard_map/dot_general | solution.py:21
  87.9 0.0 copy-start.3
  87.9 1.8 copy-done.3
  89.7 0.0 copy-start.5
  89.7 0.0 copy-start.6
  89.7 0.1 constant_dynamic-slice_fusion.1
  89.9 0.1 collective-permute-start
  90.0 0.8 copy-done.5
  90.8 0.1 copy-done.6
  90.9 1.0 pad_maximum_fusion.2
  91.9 0.0 all-gather.4.cloned.1.call-update
  91.9 0.0 all-gather.8.cloned.1.call-start
  92.0 1.9 collective-permute-done
  93.9 2.4 dynamic-slice_add_fusion
  96.2 0.1 constant_dynamic-slice_fusion
  96.3 2.2 collective-permute-start.1
  98.5 21.9 %collective-permute-done.1 = f32[256,896]{1,0:T(8,128)} collective-permute-done((f32[256,896]{1,0:T(8,128)S(1)}, f32[256,896]{1,0:T(8,128)}, u32[]{:S(2)}, u32[]{:S(2)}) %collective-permute-start.1) | collective-permute-done | bytes 917536 | tf_op jit(solution)/shard_map/ppermute | solution.py:45
  120.4 1.3 dynamic-slice_add_fusion.1
  121.7 2.2 collective-permute-start.2
  123.9 37.4 %collective-permute-done.2 = f32[256,896]{1,0:T(8,128)} collective-permute-done((f32[256,896]{1,0:T(8,128)S(1)}, f32[256,896]{1,0:T(8,128)}, u32[]{:S(2)}, u32[]{:S(2)}) %collective-permute-start.2) | collective-permute-done | bytes 917536 | tf_op jit(solution)/shard_map/ppermute | solution.py:45
  161.3 1.3 broadcast_select_fusion.3
  162.6 1.3 pad_maximum_fusion.1
  163.9 0.0 collective-permute-start.3
  163.9 0.0 all-gather.6.cloned.1.call-done
  163.9 0.0 all-gather.8.cloned.1.call-update
  164.0 4.3 %collective-permute-done.3 = f32[512,896]{1,0:T(8,128)} collective-permute-done((f32[512,896]{1,0:T(8,128)}, f32[512,896]{1,0:T(8,128)}, u32[]{:S(2)}, u32[]{:S(2)}) %collective-permute-start.3) | collective-permute-done | bytes 1835040 | tf_op jit(solution)/shard_map/ppermute | solution.py:45
  168.2 3.6 %broadcast_select_fusion.1 = (f32[512,896]{1,0:T(8,128)}, f32[512,896]{1,0:T(8,128)}) fusion(f32[512,896]{1,0:T(8,128)} %collective-permute-done.3, pred[]{:T(512)S(6)} %eq.11, f32[256,896]{1,0:T(8,128)S(1)} %get-tuple-element.11, f32[256,896]{1,0:T(8,128)S(1)} %get-tuple-element.10), kind=kLoop, calls=%fused_computation.25 | loop fusion | flops 1376256 | bytes 7340033 | tf_op jit(solution)/shard_map/jit(_where)/select_n | solution.py:57
  171.8 0.0 all-gather.4.cloned.1.call-done
  171.8 0.0 copy-start.8
  171.8 4.8 %fusion.2 = bf16[1024,896]{1,0:T(8,128)(2,1)S(1)} fusion(f32[512,896]{1,0:T(8,128)} %get-tuple-element.9, f32[512,896]{1,0:T(8,128)} %get-tuple-element.8, bf16[1024,1792]{1,0:T(8,128)(2,1)} %all-gather.4.cloned.1.call-done), kind=kLoop, calls=%fused_computation.8 | loop fusion | flops 11927552 | bytes 9175040 | tf_op jit(solution)/shard_map/convert_element_type | solution.py:15
  176.6 0.0 copy-done.8
  176.7 0.0 copy-start.4
  176.7 0.0 copy-start
  176.7 0.0 copy-start.1
  176.7 0.0 copy-start.2
  176.7 6.7 %fusion.12 = f32[1024,2048]{1,0:T(8,128)} fusion(bf16[1024,896]{1,0:T(8,128)(2,1)S(1)} %fusion.2, bf16[2048,896]{1,0:T(8,128)(2,1)S(1)} %copy-done.8), kind=kOutput, calls=%fused_computation.32 | convolution fusion | flops 3758096384 | bytes 13893632 | tf_op jit(solution)/shard_map/dot_general | solution.py:21
  183.4 0.0 copy-done.4
  183.4 0.0 copy-done
  183.4 0.0 copy-done.1
  183.4 0.0 copy-done.2
  183.5 10.7 %add_convert_fusion = bf16[1024,2048]{1,0:T(8,128)(2,1)} fusion(f32[1024,2048]{1,0:T(8,128)} %fusion.12, bf16[2048,896]{1,0:T(8,128)(2,1)} %param.12, f32[512,896]{1,0:T(8,128)S(1)} %copy-done.1, f32[512,896]{1,0:T(8,128)S(1)} %copy-done, bf16[1024,1792]{1,0:T(8,128)(2,1)S(1)} %copy-done.2), kind=kOutput, calls=%fused_computation | convolution fusion | flops 3769630720 | bytes 21757952 | tf_op jit(solution)/shard_map/dot_general | solution.py:21
  194.1 10.7 %all-to-all-start.1 = ((bf16[32,32,2048]{2,1,0:T(8,128)(2,1)}), bf16[32,32,2048]{2,1,0:T(8,128)(2,1)}, u32[]{:S(2)}, u32[]{:S(2)}) async-start(bf16[32,32,2048]{2,1,0:T(8,128)(2,1)} %bitcast.15), calls=%async_computation.1 | async-start | bytes 8388608 | tf_op jit(solution)/shard_map/all_to_all | solution.py:38
  204.8 9.4 %convolution_convert_fusion = bf16[896,2048]{1,0:T(8,128)(2,1)} fusion(bf16[1024,2048]{1,0:T(8,128)(2,1)} %bitcast, bf16[1024,1792]{1,0:T(8,128)(2,1)} %all-gather.4.cloned.1.call-done), kind=kOutput, calls=%fused_computation.18 | convolution fusion | flops 3767271424 | bytes 11534336 | tf_op jit(solution)/shard_map/dot_general | solution.py:27
  214.2 38.0 %all-gather.8.cloned.1.call-done = bf16[1024,2048]{1,0:T(8,128)(2,1)} async-done(((bf16[512,2048]{1,0:T(8,128)(2,1)}), bf16[1024,2048]{1,0:T(8,128)(2,1)}) %all-gather.8.cloned.1.call-update) | async-done | bytes 4194320 | tf_op jit(solution)/shard_map/all_gather | solution.py:89
  252.2 8.6 %convert_bitcast_fusion.1 = bf16[2048,896]{0,1:T(8,128)(2,1)} fusion(bf16[1024,896]{1,0:T(8,128)(2,1)} %copy-done.4, bf16[1024,2048]{1,0:T(8,128)(2,1)} %all-gather.8.cloned.1.call-done), kind=kOutput, calls=%fused_computation.16 | convolution fusion | flops 3759931392 | bytes 9699328 | tf_op jit(solution)/shard_map/dot_general | solution.py:27
  260.8 6.0 %copy.11 = bf16[2048,896]{1,0:T(8,128)(2,1)} copy(bf16[2048,896]{0,1:T(8,128)(2,1)} %convert_bitcast_fusion.1) | data formatting | bytes 7340032
  266.8 9.3 %convert_bitcast_fusion = bf16[2048,896]{0,1:T(8,128)(2,1)} fusion(bf16[1024,2048]{1,0:T(8,128)(2,1)} %all-gather.8.cloned.1.call-done, f32[512,896]{1,0:T(8,128)} %get-tuple-element.9, f32[512,896]{1,0:T(8,128)S(1)} %copy-done, bf16[1024,1792]{1,0:T(8,128)(2,1)} %all-gather.4.cloned.1.call-done), kind=kOutput, calls=%fused_computation.15 | convolution fusion | flops 3767271424 | bytes 13369344 | tf_op jit(solution)/shard_map/dot_general | solution.py:27
  276.1 6.0 %copy.12 = bf16[2048,896]{1,0:T(8,128)(2,1)} copy(bf16[2048,896]{0,1:T(8,128)(2,1)} %convert_bitcast_fusion) | data formatting | bytes 7340032
  282.2 0.0 all-to-all-done.1
  282.2 3.7 %reduce_sum.12 = bf16[32,2048]{1,0:T(8,128)(2,1)} reduce(bf16[32,32,2048]{2,1,0:T(8,128)(2,1)} %all-to-all-done.1, bf16[]{:T(256)} %constant.46.clone.1), dimensions={0}, to_apply=%region_0.1 | reduce | flops 2031616 | bytes 4325378 | tf_op jit(solution)/shard_map/reduce_sum | solution.py:40
Async XLA Ops:
  10.5 9.8 %copy-start.7 = (bf16[32,2048]{1,0:T(8,128)(2,1)S(1)}, bf16[32,2048]{1,0:T(8,128)(2,1)}, u32[]{:S(2)}) copy-start(bf16[32,2048]{1,0:T(8,128)(2,1)} %param.7) | copy-start | bytes 393220
  10.5 69.9 %all-to-all-start = ((bf16[32,32,2048]{2,1,0:T(8,128)(2,1)}), bf16[32,32,2048]{2,1,0:T(8,128)(2,1)}, u32[]{:S(2)}, u32[]{:S(2)}) async-start(bf16[32,32,2048]{2,1,0:T(8,128)(2,1)} %tile.2), calls=%async_computation | async-start | bytes 8388608 | tf_op jit(solution)/shard_map/all_to_all | solution.py:34
  20.3 143.6 %all-gather.6.cloned.1.call-start = ((), (), s32[]{:S(2)}) async-start(), calls=%async_computation.3 | async-start | bytes 2621440 | tf_op jit(solution)/shard_map/all_gather | solution.py:89
  80.4 91.4 %all-gather.4.cloned.1.call-start = ((), (), s32[]{:S(2)}) async-start(), calls=%async_computation.2 | async-start | bytes 4587520 | tf_op jit(solution)/shard_map/all_gather | solution.py:79
  87.9 1.8 copy-start.3
  89.7 1.0 copy-start.5
  89.7 1.2 copy-start.6
  89.9 4.0 %collective-permute-start = (f32[512,896]{1,0:T(8,128)S(1)}, f32[512,896]{1,0:T(8,128)}, u32[]{:S(2)}, u32[]{:S(2)}) collective-permute-start(f32[512,896]{1,0:T(8,128)S(1)} %constant_dynamic-slice_fusion.1), channel_id=1, source_target_pairs={{0,1},{1,0},{2,3},{3,2},{4,5},{5,4},{6,7},{7,6},{8,9},{9,8},{10,11... | collective-permute-start | bytes 5505032 | tf_op jit(solution)/shard_map/ppermute | solution.py:45
  91.9 160.3 %all-gather.8.cloned.1.call-start = ((), (), s32[]{:S(2)}) async-start(), calls=%async_computation.4 | async-start | bytes 6291456 | tf_op jit(solution)/shard_map/all_gather | solution.py:89
  96.3 24.1 %collective-permute-start.1 = (f32[256,896]{1,0:T(8,128)S(1)}, f32[256,896]{1,0:T(8,128)}, u32[]{:S(2)}, u32[]{:S(2)}) collective-permute-start(f32[256,896]{1,0:T(8,128)S(1)} %constant_dynamic-slice_fusion), channel_id=1, source_target_pairs={{0,2},{1,3},{2,0},{3,1},{4,6},{5,7},{6,4},{7,5},{8,10},{9,11},{10,... | collective-permute-start | bytes 2752520 | tf_op jit(solution)/shard_map/ppermute | solution.py:45
  121.7 39.6 %collective-permute-start.2 = (f32[256,896]{1,0:T(8,128)S(1)}, f32[256,896]{1,0:T(8,128)}, u32[]{:S(2)}, u32[]{:S(2)}) collective-permute-start(f32[256,896]{1,0:T(8,128)S(1)} %dynamic-slice_add_fusion.1), channel_id=1, source_target_pairs={{0,2},{1,3},{2,0},{3,1},{4,6},{5,7},{6,4},{7,5},{8,10},{9,11},{10,... | collective-permute-start | bytes 2752520 | tf_op jit(solution)/shard_map/ppermute | solution.py:45
  163.9 4.3 %collective-permute-start.3 = (f32[512,896]{1,0:T(8,128)}, f32[512,896]{1,0:T(8,128)}, u32[]{:S(2)}, u32[]{:S(2)}) collective-permute-start(f32[512,896]{1,0:T(8,128)} %pad_maximum_fusion.1), channel_id=1, source_target_pairs={{0,1},{1,0},{2,3},{3,2},{4,5},{5,4},{6,7},{7,6},{8,9},{9,8},{10,11... | collective-permute-start | bytes 5505032 | tf_op jit(solution)/shard_map/ppermute | solution.py:45
  171.8 4.8 %copy-start.8 = (bf16[2048,896]{1,0:T(8,128)(2,1)S(1)}, bf16[2048,896]{1,0:T(8,128)(2,1)}, u32[]{:S(2)}) copy-start(bf16[2048,896]{1,0:T(8,128)(2,1)} %param.11) | copy-start | bytes 11010052
  176.7 6.8 %copy-start.4 = (bf16[1024,896]{1,0:T(8,128)(2,1)}, bf16[1024,896]{1,0:T(8,128)(2,1)S(1)}, u32[]{:S(2)}) copy-start(bf16[1024,896]{1,0:T(8,128)(2,1)S(1)} %fusion.2) | copy-start | bytes 5505028
  176.7 6.8 %copy-start = (f32[512,896]{1,0:T(8,128)S(1)}, f32[512,896]{1,0:T(8,128)}, u32[]{:S(2)}) copy-start(f32[512,896]{1,0:T(8,128)} %get-tuple-element.8) | copy-start | bytes 5505028
  176.7 6.8 %copy-start.1 = (f32[512,896]{1,0:T(8,128)S(1)}, f32[512,896]{1,0:T(8,128)}, u32[]{:S(2)}) copy-start(f32[512,896]{1,0:T(8,128)} %get-tuple-element.9) | copy-start | bytes 5505028
  176.7 6.8 %copy-start.2 = (bf16[1024,1792]{1,0:T(8,128)(2,1)S(1)}, bf16[1024,1792]{1,0:T(8,128)(2,1)}, u32[]{:S(2)}) copy-start(bf16[1024,1792]{1,0:T(8,128)(2,1)} %all-gather.4.cloned.1.call-done) | copy-start | bytes 11010052
  194.1 88.0 %all-to-all-start.1 = ((bf16[32,32,2048]{2,1,0:T(8,128)(2,1)}), bf16[32,32,2048]{2,1,0:T(8,128)(2,1)}, u32[]{:S(2)}, u32[]{:S(2)}) async-start(bf16[32,32,2048]{2,1,0:T(8,128)(2,1)} %bitcast.15), calls=%async_computation.1 | async-start | bytes 8388608 | tf_op jit(solution)/shard_map/all_to_all | solution.py:38
Sparse Core Ops, SparseCore 0:
  80.5 34.0 all-gather.5
  116.8 49.3 all-gather.3
  167.9 84.2 all-gather.7

commit v5 on v2

--- a/solution.py
+++ b/solution.py
@@ -1,6 +1,7 @@
 import jax
 import jax.numpy as jnp
 from jax import lax
+from jax.experimental.layout import Layout, with_layout_constraint
 from jax.sharding import PartitionSpec as P
 
 
@@ -81,8 +82,9 @@
       hidden, gate_grad, up_grad = swiglu_back(hidden_total, gate_all, up_all)
       grad_down = contract_first(hidden, grad_rows).astype(jnp.bfloat16)
       input_rows = lax.all_gather(inputs, "row", axis=0, tiled=True)
-      gate_total = contract_first(input_rows, gate_grad)
-      up_total = contract_first(input_rows, up_grad)
+      row_major = Layout(major_to_minor=(0, 1))
+      gate_total = with_layout_constraint(contract_first(input_rows, gate_grad), row_major)
+      up_total = with_layout_constraint(contract_first(input_rows, up_grad), row_major)
       input_total = scatter_sum_rows(
           contract_last(gate_grad, gate_weight) + contract_last(up_grad, up_weight),
           "row",

time: 361 us -> 347 us (0.961)
  local copies, waits for them, and re-layouts: 17.5 us -> 5.44 us
    unnamed x18 -> x22, local copies, waits for them, and re-layouts: 14 us -> 1.87 us
  transfers between devices with their start and end apart: 8 -> 8, of which waited for: 6 -> 6; matrix products, arithmetic and copies ran while one was open for 22% -> 19% of each run, Pallas kernels for 0% -> 0%
where the time goes in v5:
time: 347 us; the launch traced here: 344 us
  waiting for transfers between devices  233 us (67%)
  matrix products  49.4 us (14%)
  starting transfers between devices  22.6 us (7%)
  other arithmetic  19.2 us (6%)
  between operations  14.3 us (4%)
  local copies, waits for them, and re-layouts  5.44 us (2%)
    all_gather x1, waiting for transfers between devices, body(): input_rows = lax.all_gather(inputs, 'row', axis=0, tiled=True)  112 us
    all_to_all x1, waiting for transfers between devices, gather_rows(): return lax.all_to_all(tiled, axis, 0, 0, tiled=True)  66.3 us
    ppermute x4, waiting for transfers between devices, swap(): return lax.ppermute(value, axis, pairs)  54.5 us
    dot_general x3, matrix products, contract_first(): lax.dot_general(left, right, (((0,), (0,)), ((), ())), preferred_element_...  25.1 us
    dot_general x3, matrix products, contract_last(): lax.dot_general(left, right, (((1,), (1,)), ((), ())), preferred_element_...  24.3 us
    all_to_all x1, starting transfers between devices, gather_rows(): return lax.all_to_all(tiled, axis, 0, 0, tiled=True)  9.76 us
    all_to_all x1, starting transfers between devices, scatter_sum_rows(): lax.all_to_all(partial.astype(jnp.bfloat16), axis, 0, 0, tiled=True)  8.22 us
  transfers between devices with their start and end apart: 8, of which 6 were waited for; matrix products, arithmetic and copies ran while one was open for 19% of the time, Pallas kernels for 0%

profile of v5, /device:TPU:2, one launch (start us, length us, event | category | flops | bytes accessed | tf_op | source)
XLA Modules:
  0.0 343.8 jit_solution(1445105557100770814)
XLA Ops:
  7.2 3.4 tile.2
  10.5 0.0 copy-start.7
  10.5 0.0 copy-start.8
  10.5 9.8 %all-to-all-start = ((bf16[32,32,2048]{2,1,0:T(8,128)(2,1)}), bf16[32,32,2048]{2,1,0:T(8,128)(2,1)}, u32[]{:S(2)}, u32[]{:S(2)}) async-start(bf16[32,32,2048]{2,1,0:T(8,128)(2,1)} %tile.2), calls=%async_computation | async-start | bytes 8388608 | tf_op jit(solution)/shard_map/all_to_all | solution.py:35
  20.3 0.0 all-gather.3.cloned.1.call-start
  20.4 0.0 copy-done.7
  20.4 0.0 copy-done.8
  20.4 1.0 pad_maximum_fusion.2
  21.4 0.0 all-gather.3.cloned.1.call-update
  21.4 0.0 all-gather.5.cloned.1.call-start
  21.5 66.3 %all-to-all-done = bf16[32,32,2048]{2,1,0:T(8,128)(2,1)} async-done(((bf16[32,32,2048]{2,1,0:T(8,128)(2,1)}), bf16[32,32,2048]{2,1,0:T(8,128)(2,1)}, u32[]{:S(2)}, u32[]{:S(2)}) %all-to-all-start) | async-done | bytes 4194336 | tf_op jit(solution)/shard_map/all_to_all | solution.py:35
  87.8 7.4 %fusion.11 = f32[1024,896]{1,0:T(8,128)S(1)} fusion(bf16[1024,2048]{1,0:T(8,128)(2,1)} %bitcast, bf16[896,2048]{1,0:T(8,128)(2,1)} %param.13), kind=kOutput, calls=%fused_computation.31 | convolution fusion | flops 3758096384 | bytes 11534336 | tf_op jit(solution)/shard_map/dot_general | solution.py:22
  95.2 0.0 copy-start.5
  95.2 1.8 copy-done.5
  97.0 0.1 constant_dynamic-slice_fusion.1
  97.2 0.1 collective-permute-start
  97.3 3.9 %collective-permute-done = f32[512,896]{1,0:T(8,128)} collective-permute-done((f32[512,896]{1,0:T(8,128)S(1)}, f32[512,896]{1,0:T(8,128)}, u32[]{:S(2)}, u32[]{:S(2)}) %collective-permute-start) | collective-permute-done | bytes 1835040 | tf_op jit(solution)/shard_map/ppermute | solution.py:46
  101.2 2.2 dynamic-slice_add_fusion
  103.4 0.1 constant_dynamic-slice_fusion
  103.5 2.2 collective-permute-start.1
  105.7 21.9 %collective-permute-done.1 = f32[256,896]{1,0:T(8,128)} collective-permute-done((f32[256,896]{1,0:T(8,128)S(1)}, f32[256,896]{1,0:T(8,128)}, u32[]{:S(2)}, u32[]{:S(2)}) %collective-permute-start.1) | collective-permute-done | bytes 917536 | tf_op jit(solution)/shard_map/ppermute | solution.py:46
  127.6 1.3 dynamic-slice_add_fusion.1
  128.8 2.2 collective-permute-start.2
  131.0 0.0 all-gather.5.cloned.1.call-update
  131.1 24.7 %collective-permute-done.2 = f32[256,896]{1,0:T(8,128)} collective-permute-done((f32[256,896]{1,0:T(8,128)S(1)}, f32[256,896]{1,0:T(8,128)}, u32[]{:S(2)}, u32[]{:S(2)}) %collective-permute-start.2) | collective-permute-done | bytes 917536 | tf_op jit(solution)/shard_map/ppermute | solution.py:46
  155.7 1.3 broadcast_select_fusion.3
  157.0 1.3 pad_maximum_fusion.1
  158.4 0.0 collective-permute-start.3
  158.4 4.1 %collective-permute-done.3 = f32[512,896]{1,0:T(8,128)} collective-permute-done((f32[512,896]{1,0:T(8,128)}, f32[512,896]{1,0:T(8,128)}, u32[]{:S(2)}, u32[]{:S(2)}) %collective-permute-start.3) | collective-permute-done | bytes 1835040 | tf_op jit(solution)/shard_map/ppermute | solution.py:46
  162.5 3.6 %broadcast_select_fusion.1 = (f32[512,896]{1,0:T(8,128)}, f32[512,896]{1,0:T(8,128)}) fusion(f32[512,896]{1,0:T(8,128)} %collective-permute-done.3, pred[]{:T(512)S(6)} %eq.11, f32[256,896]{1,0:T(8,128)S(1)} %get-tuple-element.7, f32[256,896]{1,0:T(8,128)S(1)} %get-tuple-element.6), kind=kLoop, calls=%fused_computation.25 | loop fusion | flops 1376256 | bytes 7340033 | tf_op jit(solution)/shard_map/jit(_where)/select_n | solution.py:58
  166.1 0.0 all-gather.3.cloned.1.call-done
  166.1 0.0 copy-start.10
  166.1 4.8 %fusion.2 = bf16[1024,896]{1,0:T(8,128)(2,1)S(1)} fusion(f32[512,896]{1,0:T(8,128)} %get-tuple-element.5, f32[512,896]{1,0:T(8,128)} %get-tuple-element.4, bf16[1024,1792]{1,0:T(8,128)(2,1)} %all-gather.3.cloned.1.call-done), kind=kLoop, calls=%fused_computation.10 | loop fusion | flops 11927552 | bytes 9175040 | tf_op jit(solution)/shard_map/convert_element_type | solution.py:16
  170.9 0.0 copy-done.10
  171.0 0.0 copy-start.6
  171.0 0.0 copy-start
  171.0 0.0 copy-start.1
  171.0 0.0 copy-start.3
  171.0 6.8 %fusion.12 = f32[1024,2048]{1,0:T(8,128)} fusion(bf16[1024,896]{1,0:T(8,128)(2,1)S(1)} %fusion.2, bf16[2048,896]{1,0:T(8,128)(2,1)S(1)} %copy-done.10), kind=kOutput, calls=%fused_computation.32 | convolution fusion | flops 3758096384 | bytes 13893632 | tf_op jit(solution)/shard_map/dot_general | solution.py:22
  177.8 0.0 copy-done.6
  177.8 0.0 copy-done
  177.8 0.0 copy-done.1
  177.8 0.0 copy-done.3
  177.9 10.0 %add_convert_fusion = bf16[1024,2048]{1,0:T(8,128)(2,1)} fusion(f32[1024,2048]{1,0:T(8,128)} %fusion.12, bf16[2048,896]{1,0:T(8,128)(2,1)} %param.12, f32[512,896]{1,0:T(8,128)S(1)} %copy-done.1, f32[512,896]{1,0:T(8,128)S(1)} %copy-done, bf16[1024,1792]{1,0:T(8,128)(2,1)S(1)} %copy-done.3), kind=kOutput, calls=%fused_computation | convolution fusion | flops 3769630720 | bytes 21757952 | tf_op jit(solution)/shard_map/dot_general | solution.py:22
  187.9 8.2 %all-to-all-start.1 = ((bf16[32,32,2048]{2,1,0:T(8,128)(2,1)}), bf16[32,32,2048]{2,1,0:T(8,128)(2,1)}, u32[]{:S(2)}, u32[]{:S(2)}) async-start(bf16[32,32,2048]{2,1,0:T(8,128)(2,1)} %bitcast.15), calls=%async_computation.1 | async-start | bytes 8388608 | tf_op jit(solution)/shard_map/all_to_all | solution.py:39
  196.1 9.4 %convolution_convert_fusion = bf16[896,2048]{1,0:T(8,128)(2,1)} fusion(bf16[1024,2048]{1,0:T(8,128)(2,1)} %bitcast, bf16[1024,1792]{1,0:T(8,128)(2,1)} %all-gather.3.cloned.1.call-done), kind=kOutput, calls=%fused_computation.18 | convolution fusion | flops 3767271424 | bytes 11534336 | tf_op jit(solution)/shard_map/dot_general | solution.py:28
  205.5 112.1 %all-gather.5.cloned.1.call-done = bf16[1024,2048]{1,0:T(8,128)(2,1)} async-done(((bf16[32,2048]{1,0:T(8,128)(2,1)}), bf16[1024,2048]{1,0:T(8,128)(2,1)}) %all-gather.5.cloned.1.call-update) | async-done | bytes 4194320 | tf_op jit(solution)/shard_map/all_gather | solution.py:84
  317.6 0.0 copy-start.2
  317.6 0.0 copy-start.4
  317.6 0.0 copy-start.9
  317.6 9.3 %bitcast_convert_fusion.1 = bf16[2048,896]{1,0:T(8,128)(2,1)} fusion(bf16[1024,896]{1,0:T(8,128)(2,1)} %copy-done.6, bf16[1024,2048]{1,0:T(8,128)(2,1)} %all-gather.5.cloned.1.call-done), kind=kOutput, calls=%fused_computation.2 | convolution fusion | flops 3759931392 | bytes 9699328 | tf_op jit(solution)/shard_map/dot_general | solution.py:28
  326.9 0.0 copy-done.2
  326.9 0.0 copy-done.4
  326.9 0.0 copy-done.9
  326.9 6.4 %bitcast_convert_fusion = bf16[2048,896]{1,0:T(8,128)(2,1)} fusion(bf16[1024,2048]{1,0:T(8,128)(2,1)S(1)} %copy-done.9, f32[512,896]{1,0:T(8,128)S(1)} %copy-done.2, f32[512,896]{1,0:T(8,128)S(1)} %copy-done, bf16[1024,1792]{1,0:T(8,128)(2,1)S(1)} %copy-done.4), kind=kOutput, calls=%fused_computation.1 | convolution fusion | flops 3767271424 | bytes 13369344 | tf_op jit(solution)/shard_map/dot_general | solution.py:28
  333.3 0.0 all-to-all-done.1
  333.3 3.7 %reduce_sum.12 = bf16[32,2048]{1,0:T(8,128)(2,1)} reduce(bf16[32,32,2048]{2,1,0:T(8,128)(2,1)} %all-to-all-done.1, bf16[]{:T(256)} %constant.44.clone.1), dimensions={0}, to_apply=%region_0.1 | reduce | flops 2031616 | bytes 4325378 | tf_op jit(solution)/shard_map/reduce_sum | solution.py:41
Async XLA Ops:
  10.5 9.8 %copy-start.7 = (bf16[256,896]{1,0:T(8,128)(2,1)S(1)}, bf16[256,896]{1,0:T(8,128)(2,1)}, u32[]{:S(2)}) copy-start(bf16[256,896]{1,0:T(8,128)(2,1)} %param.10) | copy-start | bytes 1376260
  10.5 9.8 %copy-start.8 = (bf16[256,896]{1,0:T(8,128)(2,1)S(1)}, bf16[256,896]{1,0:T(8,128)(2,1)}, u32[]{:S(2)}) copy-start(bf16[256,896]{1,0:T(8,128)(2,1)} %param.9) | copy-start | bytes 1376260
  10.5 77.2 %all-to-all-start = ((bf16[32,32,2048]{2,1,0:T(8,128)(2,1)}), bf16[32,32,2048]{2,1,0:T(8,128)(2,1)}, u32[]{:S(2)}, u32[]{:S(2)}) async-start(bf16[32,32,2048]{2,1,0:T(8,128)(2,1)} %tile.2), calls=%async_computation | async-start | bytes 8388608 | tf_op jit(solution)/shard_map/all_to_all | solution.py:35
  20.3 145.8 %all-gather.3.cloned.1.call-start = ((), (), s32[]{:S(2)}) async-start(), calls=%async_computation.2 | async-start | bytes 4587520 | tf_op jit(solution)/shard_map/all_gather | solution.py:76
  21.4 296.2 %all-gather.5.cloned.1.call-start = ((), (), s32[]{:S(2)}) async-start(), calls=%async_computation.3 | async-start | bytes 4325376 | tf_op jit(solution)/shard_map/all_gather | solution.py:84
  95.2 1.8 copy-start.5
  97.2 4.0 %collective-permute-start = (f32[512,896]{1,0:T(8,128)S(1)}, f32[512,896]{1,0:T(8,128)}, u32[]{:S(2)}, u32[]{:S(2)}) collective-permute-start(f32[512,896]{1,0:T(8,128)S(1)} %constant_dynamic-slice_fusion.1), channel_id=1, source_target_pairs={{0,1},{1,0},{2,3},{3,2},{4,5},{5,4},{6,7},{7,6},{8,9},{9,8},{10,11... | collective-permute-start | bytes 5505032 | tf_op jit(solution)/shard_map/ppermute | solution.py:46
  103.5 24.1 %collective-permute-start.1 = (f32[256,896]{1,0:T(8,128)S(1)}, f32[256,896]{1,0:T(8,128)}, u32[]{:S(2)}, u32[]{:S(2)}) collective-permute-start(f32[256,896]{1,0:T(8,128)S(1)} %constant_dynamic-slice_fusion), channel_id=1, source_target_pairs={{0,2},{1,3},{2,0},{3,1},{4,6},{5,7},{6,4},{7,5},{8,10},{9,11},{10,... | collective-permute-start | bytes 2752520 | tf_op jit(solution)/shard_map/ppermute | solution.py:46
  128.8 26.9 %collective-permute-start.2 = (f32[256,896]{1,0:T(8,128)S(1)}, f32[256,896]{1,0:T(8,128)}, u32[]{:S(2)}, u32[]{:S(2)}) collective-permute-start(f32[256,896]{1,0:T(8,128)S(1)} %dynamic-slice_add_fusion.1), channel_id=1, source_target_pairs={{0,2},{1,3},{2,0},{3,1},{4,6},{5,7},{6,4},{7,5},{8,10},{9,11},{10,... | collective-permute-start | bytes 2752520 | tf_op jit(solution)/shard_map/ppermute | solution.py:46
  158.4 4.1 %collective-permute-start.3 = (f32[512,896]{1,0:T(8,128)}, f32[512,896]{1,0:T(8,128)}, u32[]{:S(2)}, u32[]{:S(2)}) collective-permute-start(f32[512,896]{1,0:T(8,128)} %pad_maximum_fusion.1), channel_id=1, source_target_pairs={{0,1},{1,0},{2,3},{3,2},{4,5},{5,4},{6,7},{7,6},{8,9},{9,8},{10,11... | collective-permute-start | bytes 5505032 | tf_op jit(solution)/shard_map/ppermute | solution.py:46
  166.1 4.8 %copy-start.10 = (bf16[2048,896]{1,0:T(8,128)(2,1)S(1)}, bf16[2048,896]{1,0:T(8,128)(2,1)}, u32[]{:S(2)}) copy-start(bf16[2048,896]{1,0:T(8,128)(2,1)} %param.11) | copy-start | bytes 11010052
  171.0 6.9 %copy-start.6 = (bf16[1024,896]{1,0:T(8,128)(2,1)}, bf16[1024,896]{1,0:T(8,128)(2,1)S(1)}, u32[]{:S(2)}) copy-start(bf16[1024,896]{1,0:T(8,128)(2,1)S(1)} %fusion.2) | copy-start | bytes 5505028
  171.0 6.9 %copy-start = (f32[512,896]{1,0:T(8,128)S(1)}, f32[512,896]{1,0:T(8,128)}, u32[]{:S(2)}) copy-start(f32[512,896]{1,0:T(8,128)} %get-tuple-element.4) | copy-start | bytes 5505028
  171.0 6.9 %copy-start.1 = (f32[512,896]{1,0:T(8,128)S(1)}, f32[512,896]{1,0:T(8,128)}, u32[]{:S(2)}) copy-start(f32[512,896]{1,0:T(8,128)} %get-tuple-element.5) | copy-start | bytes 5505028
  171.0 6.9 %copy-start.3 = (bf16[1024,1792]{1,0:T(8,128)(2,1)S(1)}, bf16[1024,1792]{1,0:T(8,128)(2,1)}, u32[]{:S(2)}) copy-start(bf16[1024,1792]{1,0:T(8,128)(2,1)} %all-gather.3.cloned.1.call-done) | copy-start | bytes 11010052
  187.9 145.4 %all-to-all-start.1 = ((bf16[32,32,2048]{2,1,0:T(8,128)(2,1)}), bf16[32,32,2048]{2,1,0:T(8,128)(2,1)}, u32[]{:S(2)}, u32[]{:S(2)}) async-start(bf16[32,32,2048]{2,1,0:T(8,128)(2,1)} %bitcast.15), calls=%async_computation.1 | async-start | bytes 8388608 | tf_op jit(solution)/shard_map/all_to_all | solution.py:39
  317.6 9.3 %copy-start.2 = (f32[512,896]{1,0:T(8,128)S(1)}, f32[512,896]{1,0:T(8,128)}, u32[]{:S(2)}) copy-start(f32[512,896]{1,0:T(8,128)} %get-tuple-element.5) | copy-start | bytes 5505028
  317.6 9.3 %copy-start.4 = (bf16[1024,1792]{1,0:T(8,128)(2,1)S(1)}, bf16[1024,1792]{1,0:T(8,128)(2,1)}, u32[]{:S(2)}) copy-start(bf16[1024,1792]{1,0:T(8,128)(2,1)} %all-gather.3.cloned.1.call-done) | copy-start | bytes 11010052
  317.6 9.3 %copy-start.9 = (bf16[1024,2048]{1,0:T(8,128)(2,1)S(1)}, bf16[1024,2048]{1,0:T(8,128)(2,1)}, u32[]{:S(2)}) copy-start(bf16[1024,2048]{1,0:T(8,128)(2,1)} %all-gather.5.cloned.1.call-done) | copy-start | bytes 12582916
Sparse Core Ops, SparseCore 0:
  23.4 55.1 all-gather.2
  131.2 186.3 all-gather.4

commit v6 on v5

--- a/solution.py
+++ b/solution.py
@@ -55,9 +55,9 @@
 
 def double(value, axis, count, bit, own):
     other = swap(value, axis, count, bit)
-    first = jnp.where(own == 0, value, other)
-    second = jnp.where(own == 0, other, value)
-    return jnp.concatenate([first, second], axis=0)
+    half = value.shape[0]
+    whole = jnp.concatenate([value, value], axis=0)
+    return lax.dynamic_update_slice_in_dim(whole, other, (1 - own) * half, axis=0)
 
 
 def sum_all(partial, axis, count):

time: 347 us -> 347 us (level)
  other arithmetic: 19.2 us -> 14.5 us
    all_gather x1, waiting for transfers between devices: 112 us -> 117 us  [body(): input_rows = lax.all_gather(inputs, 'row', axis=0, tiled=True)]
    select_n x2 -> x0, other arithmetic: 4.89 us -> none  [double(): first = jnp.where(own == 0, value, other)]
  transfers between devices with their start and end apart: 8 -> 8, of which waited for: 6 -> 6; matrix products, arithmetic and copies ran while one was open for 19% -> 18% of each run, Pallas kernels for 0% -> 0%
where the time goes in v6:
time: 347 us; the launch traced here: 344 us
  waiting for transfers between devices  236 us (68%)
  matrix products  49.9 us (14%)
  starting transfers between devices  22.7 us (7%)
  other arithmetic  14.5 us (4%)
  between operations  14.2 us (4%)
  local copies, waits for them, and re-layouts  7.01 us (2%)
    all_gather x1, waiting for transfers between devices, body(): input_rows = lax.all_gather(inputs, 'row', axis=0, tiled=True)  117 us
    all_to_all x1, waiting for transfers between devices, gather_rows(): return lax.all_to_all(tiled, axis, 0, 0, tiled=True)  66.3 us
    ppermute x4, waiting for transfers between devices, swap(): return lax.ppermute(value, axis, pairs)  51.8 us
    dot_general x3, matrix products, contract_first(): lax.dot_general(left, right, (((0,), (0,)), ((), ())), preferred_element_...  26 us
    dot_general x3, matrix products, contract_last(): lax.dot_general(left, right, (((1,), (1,)), ((), ())), preferred_element_...  23.9 us
    all_to_all x1, starting transfers between devices, gather_rows(): return lax.all_to_all(tiled, axis, 0, 0, tiled=True)  9.75 us
    all_to_all x1, starting transfers between devices, scatter_sum_rows(): lax.all_to_all(partial.astype(jnp.bfloat16), axis, 0, 0, tiled=True)  8.29 us
  transfers between devices with their start and end apart: 8, of which 6 were waited for; matrix products, arithmetic and copies ran while one was open for 18% of the time, Pallas kernels for 0%

profile of v6, /device:TPU:2, one launch (start us, length us, event | category | flops | bytes accessed | tf_op | source)
XLA Modules:
  0.0 343.9 jit_solution(14416195529176519091)
XLA Ops:
  7.2 3.4 tile.2
  10.5 0.0 copy-start.3
  10.5 0.0 copy-start.4
  10.6 9.8 %all-to-all-start = ((bf16[32,32,2048]{2,1,0:T(8,128)(2,1)}), bf16[32,32,2048]{2,1,0:T(8,128)(2,1)}, u32[]{:S(2)}, u32[]{:S(2)}) async-start(bf16[32,32,2048]{2,1,0:T(8,128)(2,1)} %tile.2), calls=%async_computation | async-start | bytes 8388608 | tf_op jit(solution)/shard_map/all_to_all | solution.py:35
  20.3 0.0 all-gather.3.cloned.1.call-start
  20.4 0.0 copy-done.3
  20.4 0.0 copy-done.4
  20.4 1.0 pad_maximum_fusion.2
  21.4 0.0 all-gather.3.cloned.1.call-update
  21.4 0.0 all-gather.5.cloned.1.call-start
  21.5 66.3 %all-to-all-done = bf16[32,32,2048]{2,1,0:T(8,128)(2,1)} async-done(((bf16[32,32,2048]{2,1,0:T(8,128)(2,1)}), bf16[32,32,2048]{2,1,0:T(8,128)(2,1)}, u32[]{:S(2)}, u32[]{:S(2)}) %all-to-all-start) | async-done | bytes 4194336 | tf_op jit(solution)/shard_map/all_to_all | solution.py:35
  87.8 7.4 %fusion.11 = f32[1024,896]{1,0:T(8,128)S(1)} fusion(bf16[1024,2048]{1,0:T(8,128)(2,1)} %bitcast, bf16[896,2048]{1,0:T(8,128)(2,1)} %param.13), kind=kOutput, calls=%fused_computation.29 | convolution fusion | flops 3758096384 | bytes 11534336 | tf_op jit(solution)/shard_map/dot_general | solution.py:22
  95.2 0.0 copy-start.2
  95.2 1.8 copy-done.2
  97.1 0.1 constant_dynamic-slice_fusion.1
  97.2 0.1 collective-permute-start
  97.3 3.9 %collective-permute-done = f32[512,896]{1,0:T(8,128)} collective-permute-done((f32[512,896]{1,0:T(8,128)S(1)}, f32[512,896]{1,0:T(8,128)}, u32[]{:S(2)}, u32[]{:S(2)}) %collective-permute-start) | collective-permute-done | bytes 1835040 | tf_op jit(solution)/shard_map/ppermute | solution.py:46
  101.2 2.2 dynamic-slice_add_fusion
  103.4 0.1 constant_dynamic-slice_fusion
  103.5 2.2 collective-permute-start.1
  105.7 21.9 %collective-permute-done.1 = f32[256,896]{1,0:T(8,128)} collective-permute-done((f32[256,896]{1,0:T(8,128)S(1)}, f32[256,896]{1,0:T(8,128)}, u32[]{:S(2)}, u32[]{:S(2)}) %collective-permute-start.1) | collective-permute-done | bytes 917536 | tf_op jit(solution)/shard_map/ppermute | solution.py:46
  127.6 1.3 dynamic-slice_add_fusion.1
  128.8 2.2 collective-permute-start.2
  131.0 0.0 all-gather.5.cloned.1.call-update
  131.1 0.1 pad_maximum_fusion.1
  131.2 24.5 %collective-permute-done.2 = f32[256,896]{1,0:T(8,128)S(1)} collective-permute-done((f32[256,896]{1,0:T(8,128)S(1)}, f32[256,896]{1,0:T(8,128)S(1)}, u32[]{:S(2)}, u32[]{:S(2)}) %collective-permute-start.2) | collective-permute-done | bytes 917536 | tf_op jit(solution)/shard_map/ppermute | solution.py:46
  155.6 0.1 constant_dynamic-update-slice_fusion.1
  155.7 0.1 collective-permute-start.3
  155.8 2.1 pad_maximum_fusion
  157.9 1.6 collective-permute-done.3
  159.6 1.3 constant_dynamic-update-slice_fusion
  160.9 0.0 all-gather.3.cloned.1.call-done
  160.9 0.0 copy-start.6
  160.9 4.1 %fusion.2 = bf16[1024,896]{1,0:T(8,128)(2,1)S(1)} fusion(f32[1024,896]{1,0:T(8,128)} %constant_dynamic-update-slice_fusion, bf16[1024,1792]{1,0:T(8,128)(2,1)} %all-gather.3.cloned.1.call-done), kind=kLoop, calls=%fused_computation.10 | loop fusion | flops 11010048 | bytes 9175040 | tf_op jit(solution)/shard_map/convert_element_type | solution.py:16
  165.0 0.2 copy-done.6
  165.2 0.0 copy-start
  165.2 0.0 copy-start.7
  165.2 6.7 %fusion.12 = f32[1024,2048]{1,0:T(8,128)} fusion(bf16[1024,896]{1,0:T(8,128)(2,1)S(1)} %fusion.2, bf16[2048,896]{1,0:T(8,128)(2,1)S(1)} %copy-done.6), kind=kOutput, calls=%fused_computation.30 | convolution fusion | flops 3758096384 | bytes 13893632 | tf_op jit(solution)/shard_map/dot_general | solution.py:22
  171.9 0.0 copy-done
  171.9 0.0 copy-done.7
  171.9 9.7 %add_convert_fusion = bf16[1024,2048]{1,0:T(8,128)(2,1)} fusion(f32[1024,2048]{1,0:T(8,128)} %fusion.12, bf16[2048,896]{1,0:T(8,128)(2,1)S(1)} %copy-done.7, f32[1024,896]{1,0:T(8,128)} %constant_dynamic-update-slice_fusion, bf16[1024,1792]{1,0:T(8,128)(2,1)S(1)} %copy-done), kind=kOutput, calls=%fused_computation | convolution fusion | flops 3768713216 | bytes 21757952 | tf_op jit(solution)/shard_map/dot_general | solution.py:22
  181.7 8.3 %all-to-all-start.1 = ((bf16[32,32,2048]{2,1,0:T(8,128)(2,1)}), bf16[32,32,2048]{2,1,0:T(8,128)(2,1)}, u32[]{:S(2)}, u32[]{:S(2)}) async-start(bf16[32,32,2048]{2,1,0:T(8,128)(2,1)} %bitcast.15), calls=%async_computation.1 | async-start | bytes 8388608 | tf_op jit(solution)/shard_map/all_to_all | solution.py:39
  190.0 9.4 %convolution_convert_fusion = bf16[896,2048]{1,0:T(8,128)(2,1)} fusion(bf16[1024,2048]{1,0:T(8,128)(2,1)} %bitcast, bf16[1024,1792]{1,0:T(8,128)(2,1)} %all-gather.3.cloned.1.call-done), kind=kOutput, calls=%fused_computation.18 | convolution fusion | flops 3767271424 | bytes 11534336 | tf_op jit(solution)/shard_map/dot_general | solution.py:28
  199.4 117.4 %all-gather.5.cloned.1.call-done = bf16[1024,2048]{1,0:T(8,128)(2,1)} async-done(((bf16[32,2048]{1,0:T(8,128)(2,1)}), bf16[1024,2048]{1,0:T(8,128)(2,1)}) %all-gather.5.cloned.1.call-update) | async-done | bytes 4194320 | tf_op jit(solution)/shard_map/all_gather | solution.py:84
  316.8 0.0 copy-start.1
  316.8 0.0 copy-start.5
  316.8 8.3 %bitcast_convert_fusion.1 = bf16[2048,896]{1,0:T(8,128)(2,1)} fusion(bf16[1024,896]{1,0:T(8,128)(2,1)S(1)} %fusion.2, bf16[1024,2048]{1,0:T(8,128)(2,1)} %all-gather.5.cloned.1.call-done), kind=kOutput, calls=%fused_computation.2 | convolution fusion | flops 3759931392 | bytes 9699328 | tf_op jit(solution)/shard_map/dot_general | solution.py:28
  325.1 0.0 copy-done.1
  325.1 0.0 copy-done.5
  325.1 8.3 %bitcast_convert_fusion = bf16[2048,896]{1,0:T(8,128)(2,1)} fusion(bf16[1024,2048]{1,0:T(8,128)(2,1)S(1)} %copy-done.5, f32[1024,896]{1,0:T(8,128)} %constant_dynamic-update-slice_fusion, bf16[1024,1792]{1,0:T(8,128)(2,1)S(1)} %copy-done.1), kind=kOutput, calls=%fused_computation.1 | convolution fusion | flops 3766353920 | bytes 13369344 | tf_op jit(solution)/shard_map/dot_general | solution.py:28
  333.4 0.0 all-to-all-done.1
  333.4 3.7 %reduce_sum.12 = bf16[32,2048]{1,0:T(8,128)(2,1)} reduce(bf16[32,32,2048]{2,1,0:T(8,128)(2,1)} %all-to-all-done.1, bf16[]{:T(256)} %constant.44.clone.1), dimensions={0}, to_apply=%region_0.1 | reduce | flops 2031616 | bytes 4325378 | tf_op jit(solution)/shard_map/reduce_sum | solution.py:41
Async XLA Ops:
  10.5 9.8 %copy-start.3 = (bf16[256,896]{1,0:T(8,128)(2,1)S(1)}, bf16[256,896]{1,0:T(8,128)(2,1)}, u32[]{:S(2)}) copy-start(bf16[256,896]{1,0:T(8,128)(2,1)} %param.10) | copy-start | bytes 1376260
  10.5 9.8 %copy-start.4 = (bf16[256,896]{1,0:T(8,128)(2,1)S(1)}, bf16[256,896]{1,0:T(8,128)(2,1)}, u32[]{:S(2)}) copy-start(bf16[256,896]{1,0:T(8,128)(2,1)} %param.9) | copy-start | bytes 1376260
  10.6 77.2 %all-to-all-start = ((bf16[32,32,2048]{2,1,0:T(8,128)(2,1)}), bf16[32,32,2048]{2,1,0:T(8,128)(2,1)}, u32[]{:S(2)}, u32[]{:S(2)}) async-start(bf16[32,32,2048]{2,1,0:T(8,128)(2,1)} %tile.2), calls=%async_computation | async-start | bytes 8388608 | tf_op jit(solution)/shard_map/all_to_all | solution.py:35
  20.3 140.6 %all-gather.3.cloned.1.call-start = ((), (), s32[]{:S(2)}) async-start(), calls=%async_computation.2 | async-start | bytes 4587520 | tf_op jit(solution)/shard_map/all_gather | solution.py:76
  21.4 295.4 %all-gather.5.cloned.1.call-start = ((), (), s32[]{:S(2)}) async-start(), calls=%async_computation.3 | async-start | bytes 4325376 | tf_op jit(solution)/shard_map/all_gather | solution.py:84
  95.2 1.8 copy-start.2
  97.2 4.0 %collective-permute-start = (f32[512,896]{1,0:T(8,128)S(1)}, f32[512,896]{1,0:T(8,128)}, u32[]{:S(2)}, u32[]{:S(2)}) collective-permute-start(f32[512,896]{1,0:T(8,128)S(1)} %constant_dynamic-slice_fusion.1), channel_id=1, source_target_pairs={{0,1},{1,0},{2,3},{3,2},{4,5},{5,4},{6,7},{7,6},{8,9},{9,8},{10,11... | collective-permute-start | bytes 5505032 | tf_op jit(solution)/shard_map/ppermute | solution.py:46
  103.5 24.1 %collective-permute-start.1 = (f32[256,896]{1,0:T(8,128)S(1)}, f32[256,896]{1,0:T(8,128)}, u32[]{:S(2)}, u32[]{:S(2)}) collective-permute-start(f32[256,896]{1,0:T(8,128)S(1)} %constant_dynamic-slice_fusion), channel_id=1, source_target_pairs={{0,2},{1,3},{2,0},{3,1},{4,6},{5,7},{6,4},{7,5},{8,10},{9,11},{10,... | collective-permute-start | bytes 2752520 | tf_op jit(solution)/shard_map/ppermute | solution.py:46
  128.8 26.8 %collective-permute-start.2 = (f32[256,896]{1,0:T(8,128)S(1)}, f32[256,896]{1,0:T(8,128)S(1)}, u32[]{:S(2)}, u32[]{:S(2)}) collective-permute-start(f32[256,896]{1,0:T(8,128)S(1)} %dynamic-slice_add_fusion.1), channel_id=1, source_target_pairs={{0,2},{1,3},{2,0},{3,1},{4,6},{5,7},{6,4},{7,5},{8,10},{9,11},{10,... | collective-permute-start | bytes 2752520 | tf_op jit(solution)/shard_map/ppermute | solution.py:46
  155.7 3.9 %collective-permute-start.3 = (f32[512,896]{1,0:T(8,128)S(1)}, f32[512,896]{1,0:T(8,128)S(1)}, u32[]{:S(2)}, u32[]{:S(2)}) collective-permute-start(f32[512,896]{1,0:T(8,128)S(1)} %constant_dynamic-update-slice_fusion.1), channel_id=1, source_target_pairs={{0,1},{1,0},{2,3},{3,2},{4,5},{5,4},{6,7},{7,6},{8,9},{9,8},{10,11... | collective-permute-start | bytes 5505032 | tf_op jit(solution)/shard_map/ppermute | solution.py:46
  160.9 4.3 %copy-start.6 = (bf16[2048,896]{1,0:T(8,128)(2,1)S(1)}, bf16[2048,896]{1,0:T(8,128)(2,1)}, u32[]{:S(2)}) copy-start(bf16[2048,896]{1,0:T(8,128)(2,1)} %param.11) | copy-start | bytes 11010052
  165.2 6.7 %copy-start = (bf16[1024,1792]{1,0:T(8,128)(2,1)S(1)}, bf16[1024,1792]{1,0:T(8,128)(2,1)}, u32[]{:S(2)}) copy-start(bf16[1024,1792]{1,0:T(8,128)(2,1)} %all-gather.3.cloned.1.call-done) | copy-start | bytes 11010052
  165.2 6.7 %copy-start.7 = (bf16[2048,896]{1,0:T(8,128)(2,1)S(1)}, bf16[2048,896]{1,0:T(8,128)(2,1)}, u32[]{:S(2)}) copy-start(bf16[2048,896]{1,0:T(8,128)(2,1)} %param.12) | copy-start | bytes 11010052
  181.7 151.7 %all-to-all-start.1 = ((bf16[32,32,2048]{2,1,0:T(8,128)(2,1)}), bf16[32,32,2048]{2,1,0:T(8,128)(2,1)}, u32[]{:S(2)}, u32[]{:S(2)}) async-start(bf16[32,32,2048]{2,1,0:T(8,128)(2,1)} %bitcast.15), calls=%async_computation.1 | async-start | bytes 8388608 | tf_op jit(solution)/shard_map/all_to_all | solution.py:39
  316.8 8.3 %copy-start.1 = (bf16[1024,1792]{1,0:T(8,128)(2,1)S(1)}, bf16[1024,1792]{1,0:T(8,128)(2,1)}, u32[]{:S(2)}) copy-start(bf16[1024,1792]{1,0:T(8,128)(2,1)} %all-gather.3.cloned.1.call-done) | copy-start | bytes 11010052
  316.8 8.3 %copy-start.5 = (bf16[1024,2048]{1,0:T(8,128)(2,1)S(1)}, bf16[1024,2048]{1,0:T(8,128)(2,1)}, u32[]{:S(2)}) copy-start(bf16[1024,2048]{1,0:T(8,128)(2,1)} %all-gather.5.cloned.1.call-done) | copy-start | bytes 12582916
Sparse Core Ops, SparseCore 0:
  23.4 55.1 all-gather.2
  131.2 185.5 all-gather.4
